TPU v7x, 128 devices: a whole 4x4x4 slice. The times are simulated.
128 devices in a mesh: ctx: 16 (over y, x), grp: 8 (over z, core).
Axes of the slice: x: 4, y: 4, z: 4, core: 2. Of those that a mesh axis runs over, the one named last changes fastest.
Arguments:
- residual: bfloat16 [8, 2048, 2880], P('grp', 'ctx'), may hold values from -3 to 3
- queries: bfloat16 [8, 2048, 2048], P('grp', 'ctx'), may hold values from -8 to 8
- stretch_kv: bfloat16 [8, 2048, 1024], P('grp', 'ctx'), may hold values from -8 to 8
- cache_kv: bfloat16 [8, 4096, 1024], P('grp', 'ctx'), may hold values from -6 to 6
- doc_lengths: int32 [8, 8], P('grp'), may hold values from 1 to 3072, 6144 in all within a row
- sinks: float32 [32], replicated, may hold values from 2 to 6
- out_proj: bfloat16 [2048, 2880], P('ctx'), may hold values from -0.75 to 0.75
- norm_gain: float32 [2880], replicated, may hold values from 0.1 to 1.9
- router: bfloat16 [2880, 64], replicated, may hold values from -0.109375 to 0.109375
- expert_ids: int32 [8, 2048, 4], P('grp', 'ctx'), may hold values from 0 to 63, all different within a row; in each aligned block of 128 rows (0 to 127, 128 to 255, ..., all dimensions but the last counted through in order) at most 10 rows name the same one
- expert_in: bfloat16 [128, 2880, 1536], P(('ctx', 'grp')), may hold values from -0.109375 to 0.109375
- expert_out: bfloat16 [128, 768, 2880], P(('ctx', 'grp')), may hold values from -0.15625 to 0.15625
Outputs:
- resid_mid: bfloat16 [8, 2048, 2880], P('grp', 'ctx')
- layer_out: bfloat16 [8, 2048, 2880], P('grp', 'ctx')
Inputs may be any that keep to these rules, and one draw needn't show every extreme that they name: `expert_ids`: in the rows of one device (aligned blocks of 128 tokens, sequence after sequence), each expert is named by at most 10 rows, and in some blocks one expert by exactly 10; a token's 4 experts differ. `doc_lengths`: A sequence's 8 lengths sum to 6144; the longest is exactly 3072.
All inputs are finite; a program needn't handle non-finite values.
Results may differ from a plain program's by a relative error of at most 0.015.
Values may be sent and summed in bfloat16 or wider, within the bound.
No kernel may reach another device: no remote copies, remote signals or barrier semaphores. Data moves between devices by JAX's collectives and lax.ppermute only.
A program may use at most 128 MiB of HBM per device.

v0:
```python
import math

import jax
import jax.numpy as jnp
from jax import lax
from jax.experimental import pallas as pl
from jax.experimental.pallas import tpu as pltpu
from jax.sharding import PartitionSpec as P

HEADS = 32
KVH = 8
HD = 64
CACHE_TK = 256


def flash_pairs(qpad, qpos, qstart, sink_rows, kv_all, cache_rows, bounds, scale):
    pairs, rows, lanes = qpad.shape
    sources, span, width = kv_all.shape
    stretch_rows = span - cache_rows
    cache_steps = cache_rows // CACHE_TK
    n_cache = sources * cache_steps
    n_blocks = n_cache + sources
    v_off = width // lanes // 2

    def block_of(j, s):
        return jnp.minimum(s[0] + j, s[1])

    def kernel(s_ref, q_ref, qpos_ref, qstart_ref, sink_ref, ck_ref, cv_ref, sk_ref, sv_ref, o_ref, m_sc, l_sc, acc_sc):
        j = pl.program_id(1)
        b = s_ref[0] + j

        @pl.when(j == 0)
        def _():
            m_sc[...] = sink_ref[...]
            l_sc[...] = jnp.zeros_like(l_sc)
            acc_sc[...] = jnp.zeros_like(acc_sc)

        def step(k_ref, v_ref, first, count):
            s = lax.dot_general(
                q_ref[...], k_ref[...], (((1,), (1,)), ((), ())), preferred_element_type=jnp.float32
            ) * scale
            kpos = first + lax.broadcasted_iota(jnp.int32, (1, count), 1)
            allowed = (kpos <= qpos_ref[...]) & (kpos >= qstart_ref[...])
            m_prev = m_sc[...]
            m_new = jnp.maximum(m_prev, jnp.max(jnp.where(allowed, s, -jnp.inf), axis=1, keepdims=True))
            p = jnp.where(allowed, jnp.exp(s - m_new), 0.0)
            shrink = jnp.exp(m_prev - m_new)
            l_sc[...] = l_sc[...] * shrink + jnp.sum(p, axis=1, keepdims=True)
            acc_sc[...] = acc_sc[...] * shrink + jnp.dot(
                p.astype(jnp.bfloat16), v_ref[...], preferred_element_type=jnp.float32
            )
            m_sc[...] = m_new

        live = b <= s_ref[1]

        @pl.when(live & (b < n_cache))
        def _():
            step(ck_ref, cv_ref, b * CACHE_TK, CACHE_TK)

        @pl.when(live & (b >= n_cache))
        def _():
            step(sk_ref, sv_ref, sources * cache_rows + (b - n_cache) * stretch_rows, stretch_rows)

        @pl.when(j == pl.num_programs(1) - 1)
        def _():
            denom = l_sc[...] + jnp.exp(sink_ref[...] - m_sc[...])
            o_ref[...] = (acc_sc[...] / denom).astype(o_ref.dtype)

    def cache_at(j, s):
        c = jnp.minimum(block_of(j, s), n_cache - 1)
        return c // cache_steps, c % cache_steps

    def cache_k(p, j, s):
        src, part = cache_at(j, s)
        return (src, part, p)

    def cache_v(p, j, s):
        src, part = cache_at(j, s)
        return (src, part, v_off + p)

    def stretch_k(p, j, s):
        return (jnp.maximum(block_of(j, s) - n_cache, 0), cache_rows // stretch_rows, p)

    def stretch_v(p, j, s):
        return (jnp.maximum(block_of(j, s) - n_cache, 0), cache_rows // stretch_rows, v_off + p)

    grid_spec = pltpu.PrefetchScalarGridSpec(
        num_scalar_prefetch=1,
        grid=(pairs, n_blocks),
        in_specs=[
            pl.BlockSpec((None, rows, lanes), lambda p, j, s: (p, 0, 0)),
            pl.BlockSpec((rows, 1), lambda p, j, s: (0, 0)),
            pl.BlockSpec((rows, 1), lambda p, j, s: (0, 0)),
            pl.BlockSpec((None, rows, 1), lambda p, j, s: (p, 0, 0)),
            pl.BlockSpec((None, CACHE_TK, lanes), cache_k),
            pl.BlockSpec((None, CACHE_TK, lanes), cache_v),
            pl.BlockSpec((None, stretch_rows, lanes), stretch_k),
            pl.BlockSpec((None, stretch_rows, lanes), stretch_v),
        ],
        out_specs=pl.BlockSpec((None, rows, lanes), lambda p, j, s: (p, 0, 0)),
        scratch_shapes=[
            pltpu.VMEM((rows, 1), jnp.float32),
            pltpu.VMEM((rows, 1), jnp.float32),
            pltpu.VMEM((rows, lanes), jnp.float32),
        ],
    )
    keys = sources * span
    return pl.pallas_call(
        kernel,
        grid_spec=grid_spec,
        out_shape=jax.ShapeDtypeStruct((pairs, rows, lanes), jnp.bfloat16),
        compiler_params=pltpu.CompilerParams(dimension_semantics=("arbitrary", "arbitrary")),
        cost_estimate=pl.CostEstimate(
            flops=2 * pairs * rows * lanes * keys,
            transcendentals=pairs * rows * keys // 2,
            bytes_accessed=2 * kv_all.size + 4 * qpad.size,
        ),
    )(bounds, qpad, qpos, qstart, sink_rows, kv_all, kv_all, kv_all, kv_all)


def attention(queries_local, kv_all, cache_rows, sinks, query_pos, query_start):
    tokens = queries_local.shape[0]
    groups = HEADS // KVH
    pairs = KVH // 2
    sources, span, _ = kv_all.shape
    q6 = queries_local.reshape(tokens, pairs, 2, groups, HD).transpose(1, 2, 3, 0, 4)
    zeros = jnp.zeros_like(q6[:, 0])
    qpad = jnp.stack(
        [jnp.concatenate([q6[:, 0], zeros], axis=-1), jnp.concatenate([zeros, q6[:, 1]], axis=-1)], axis=1
    ).reshape(pairs, 2 * groups * tokens, 2 * HD)
    rows = 2 * groups * tokens
    qpos = jnp.tile(query_pos, 2 * groups).reshape(rows, 1)
    qstart = jnp.tile(query_start, 2 * groups).reshape(rows, 1)
    sink_rows = jnp.repeat(sinks.reshape(pairs, 2 * groups), tokens, axis=1).reshape(pairs, rows, 1)
    cache_end = sources * cache_rows
    stretch_rows = span - cache_rows
    low = query_start[0]
    first = jnp.where(
        low < cache_end, low // CACHE_TK, sources * (cache_rows // CACHE_TK) + (low - cache_end) // stretch_rows
    )
    last = sources * (cache_rows // CACHE_TK) + (query_pos[-1] - cache_end) // stretch_rows
    bounds = jnp.stack([first, last]).astype(jnp.int32)
    out = flash_pairs(qpad, qpos, qstart, sink_rows, kv_all, cache_rows, bounds, 1.0 / math.sqrt(HD))
    o6 = out.reshape(pairs, 2, groups, tokens, 2, HD)
    picked = jnp.stack([o6[:, 0, :, :, 0], o6[:, 1, :, :, 1]], axis=1)
    return picked.transpose(3, 0, 1, 2, 4).reshape(tokens, HEADS * HD)


def doc_index(positions, lengths):
    ends = jnp.cumsum(lengths)
    return jnp.sum((positions[:, None] >= ends[None, :]).astype(jnp.int32), axis=1)


def gated_act(pre, half_width):
    gate = pre[:, :half_width]
    upper = pre[:, half_width:]
    return ((upper + 1.0) * gate * jax.nn.sigmoid(1.702 * gate)).astype(jnp.bfloat16)


def body(
    residual,
    queries,
    stretch_kv,
    cache_kv,
    doc_lengths,
    sinks,
    out_proj,
    norm_gain,
    router,
    expert_ids,
    expert_in,
    expert_out,
):
    tokens = residual.shape[1]
    width = residual.shape[2]
    cache_rows = cache_kv.shape[1]
    kv_cols = stretch_kv.shape[2] // 2
    groups = HEADS // KVH
    ctx_count = lax.axis_size("ctx")
    ctx_here = lax.axis_index("ctx")
    stretch_base = cache_rows * ctx_count
    span = cache_rows + tokens
    query_pos = stretch_base + ctx_here * tokens + jnp.arange(tokens, dtype=jnp.int32)
    lengths = doc_lengths[0]
    ends = jnp.cumsum(lengths)
    query_start = jnp.max(
        jnp.where(ends[None, :] <= query_pos[:, None], ends[None, :], 0), axis=1
    ).astype(jnp.int32)
    local_kv = jnp.concatenate([cache_kv[0], stretch_kv[0]], axis=0)
    kv_all = lax.all_gather(local_kv, "ctx", axis=0, tiled=False)
    attended = attention(queries[0], kv_all, cache_rows, sinks, query_pos, query_start)
    grp_here = lax.axis_index("grp")
    parity = grp_here % 2
    grp_count = lax.axis_size("grp")
    pair_perm = [(g, g ^ 1) for g in range(grp_count)]
    head_rows = out_proj.shape[0] // 2
    proj_half = lax.all_gather(
        lax.dynamic_slice_in_dim(out_proj, parity * head_rows, head_rows, 0), "ctx", axis=0, tiled=True
    )
    by_parity = attended.reshape(tokens, HEADS // 2, 2, HD)
    mine = jnp.where(parity == 0, by_parity[:, :, 0], by_parity[:, :, 1]).reshape(tokens, -1)
    theirs_cols = jnp.where(parity == 0, by_parity[:, :, 1], by_parity[:, :, 0]).reshape(tokens, -1)
    partner_cols = lax.ppermute(theirs_cols, "grp", pair_perm)
    both = jnp.dot(
        jnp.concatenate([mine, partner_cols], axis=0), proj_half, preferred_element_type=jnp.float32
    )
    back = lax.ppermute(both[tokens:], "grp", pair_perm)
    projected = both[:tokens] + back
    mid = (residual[0].astype(jnp.float32) + projected).astype(jnp.bfloat16)
    mid_float = mid.astype(jnp.float32)
    normed = (
        mid_float
        * lax.rsqrt(jnp.mean(mid_float * mid_float, axis=-1, keepdims=True) + 1e-05)
        * norm_gain
    ).astype(jnp.bfloat16)
    logits = jnp.dot(normed, router, preferred_element_type=jnp.float32)
    experts = router.shape[1]
    chosen_ids = expert_ids[0]
    topk = chosen_ids.shape[1]
    picks = chosen_ids[:, :, None] == jnp.arange(experts, dtype=jnp.int32)[None, None, :]
    chosen = jnp.sum(jnp.where(picks, logits[:, None, :], 0.0), axis=-1)
    raised = jnp.exp(chosen)
    route_weights = raised / jnp.sum(raised, axis=-1, keepdims=True)
    capacity = 2 * ((5 * tokens * topk + 8 * experts - 1) // (8 * experts))
    owners = 2 * experts
    half_cap = capacity // 2
    flat_ids = chosen_ids.reshape(-1)
    pairs = flat_ids.shape[0]
    onehot = (flat_ids[:, None] == jnp.arange(experts, dtype=jnp.int32)[None, :]).astype(jnp.int32)
    slots = jnp.sum(onehot * (jnp.cumsum(onehot, axis=0) - 1), axis=1)
    dest = (slots % half_cap) * owners + 2 * flat_ids + slots // half_cap
    source_rows = jnp.arange(pairs, dtype=jnp.int32) // topk
    slot_source = jnp.zeros((owners * half_cap,), jnp.int32).at[dest].set(source_rows)
    split = normed[slot_source].reshape(half_cap, owners, width)
    in_weights = expert_in[0]
    out_weights = expert_out[0]
    half_width = out_weights.shape[0]
    received = lax.all_to_all(split, ("ctx", "grp"), split_axis=1, concat_axis=1, tiled=True)
    partner_rows = lax.ppermute(received, "grp", pair_perm)

    def expert_half(rows):
        pre = jnp.dot(rows.reshape(-1, width), in_weights, preferred_element_type=jnp.float32)
        hidden = gated_act(pre, half_width)
        return jnp.dot(hidden, out_weights, preferred_element_type=jnp.float32).astype(jnp.bfloat16)

    own_part = expert_half(received)
    partner_part = expert_half(partner_rows)
    partner_back = lax.ppermute(partner_part, "grp", pair_perm)
    summed = (own_part.astype(jnp.float32) + partner_back.astype(jnp.float32)).astype(jnp.bfloat16)
    returned = lax.all_to_all(
        summed.reshape(half_cap, owners, width), ("ctx", "grp"), split_axis=1, concat_axis=1, tiled=True
    )
    expert_rows = returned.reshape(owners * half_cap, width)
    pair_dest = dest.reshape(tokens, topk)
    mixture = mid_float
    for k in range(topk):
        mixture = mixture + expert_rows[pair_dest[:, k]].astype(jnp.float32) * route_weights[:, k:k + 1]
    final = mixture.astype(jnp.bfloat16)
    return (mid[None], final[None])


def solution(mesh):
    return jax.shard_map(
        body,
        mesh=mesh,
        in_specs=(
            P("grp", "ctx", None),
            P("grp", "ctx", None),
            P("grp", "ctx", None),
            P("grp", "ctx", None),
            P("grp", None),
            P(),
            P("ctx", None),
            P(),
            P(),
            P("grp", "ctx", None),
            P(("ctx", "grp"), None, None),
            P(("ctx", "grp"), None, None),
        ),
        out_specs=(P("grp", "ctx", None), P("grp", "ctx", None)),
        check_vma=False,
    )
```

profile of v0, /device:TPU:1, one launch (start us, length us, event | category | flops | bytes accessed | tf_op | source)
XLA Modules:
  0.0 497.5 jit_solution(2853111968621308454)
XLA Ops:
  7.2 2.2 pad_maximum_fusion.1
  13.2 1.3 copy.127
  16.8 3.3 reshape_reshape.8.sink_ref
  20.6 82.7 %all-gather.6.cloned.1.call-done = bf16[6144,1024]{1,0:T(8,128)(2,1)} async-done(((bf16[384,1024]{1,0:T(8,128)(2,1)}), bf16[6144,1024]{1,0:T(8,128)(2,1)}) %all-gather.6.cloned.1.call-update) | async-done | bytes 12582928 | tf_op jit(solution)/shard_map/all_gather | solution.py:190
  103.3 32.1 %shard_map.131 = bf16[4,1024,128]{2,1,0:T(8,128)(2,1)} custom-call(s32[2]{0:T(128)} %pad_add_fusion.s_ref, bf16[4,1024,128]{2,1,0:T(8,128)(2,1)} %bitcast.107, s32[1024,1]{1,0:T(8,128)} %copy.128.qpos_ref, s32[1024,1]{1,0:T(8,128)} %copy.129.qstart_ref, f32[4,1024,1]{2,1,0:T(8,128)} %reshape_reshape.8.sink_ref, bf16[16,384,1024]{2,1,0:T(8,128)(2,1)} %bitcast.98, ...), custom_call_target="tpu_custom_call" | custom-call | flops 6442450944 | bytes 14680064 | tf_op jit(solution)/shard_map/pallas_call | solution.py:108
  135.4 1.5 copy.131
  138.5 29.2 %collective-permute-start = (bf16[128,1024]{0,1:T(8,128)(2,1)S(1)}, bf16[128,1024]{0,1:T(8,128)(2,1)S(1)}, u32[]{:S(2)}, u32[]{:S(2)}) collective-permute-start(bf16[128,1024]{0,1:T(8,128)(2,1)S(1)} %bitcast.116), channel_id=1, source_target_pairs={{0,1},{1,0},{2,3},{3,2},{4,5},{5,4},{6,7},{7,6},{8,9},{9,8},{10,11... | collective-permute-start | bytes 786440 | tf_op jit(solution)/shard_map/ppermute | solution.py:203
  169.2 5.3 %fusion.30 = f32[256,2880]{0,1:T(8,128)S(1)} fusion(bf16[1024,2880]{1,0:T(8,128)(2,1)} %all-gather.4.cloned.1.call-done, bf16[128,1024]{0,1:T(8,128)(2,1)S(1)} %collective-permute-done, bf16[128,1024]{0,1:T(8,128)(2,1)S(1)} %bitcast.115), kind=kOutput, calls=%fused_computation.44 | convolution fusion | flops 1510998016 | bytes 9371648 | tf_op jit(solution)/shard_map/dot_general | solution.py:204
  174.4 1.6 copy-done.3
  178.2 2.4 scatter_custom_fusion
  180.9 2.0 fusion.14
  183.7 4.6 gather_fusion
  188.3 4.2 copy.141
  192.5 123.5 %all_to_all.10 = bf16[5,128,2880]{2,0,1:T(8,128)(2,1)} all-to-all(bf16[5,128,2880]{2,0,1:T(8,128)(2,1)S(1)} %copy.141), channel_id=1, replica_groups=mesh['ctx'=16,'grp'=8] {'ctx','grp'}, dimensions={1} | all-to-all | bytes 7372800 | tf_op jit(solution)/shard_map/all_to_all | solution.py:238
  316.0 7.9 %copy.143 = bf16[5,128,2880]{1,2,0:T(8,128)(2,1)} copy(bf16[5,128,2880]{2,0,1:T(8,128)(2,1)} %all_to_all.10) | data formatting | bytes 7372800 | tf_op jit(solution)/shard_map/all_to_all | solution.py:238
  323.9 1.4 collective-permute-start.2
  325.3 6.4 %collective-permute-done.2 = bf16[5,128,2880]{1,2,0:T(8,128)(2,1)} collective-permute-done((bf16[5,128,2880]{1,2,0:T(8,128)(2,1)}, bf16[5,128,2880]{1,2,0:T(8,128)(2,1)}, u32[]{:S(2)}, u32[]{:S(2)}) %collective-permute-start.2) | collective-permute-done | bytes 3686432 | tf_op jit(solution)/shard_map/ppermute | solution.py:239
  331.7 6.3 %copy.144 = bf16[5,128,2880]{2,1,0:T(8,128)(2,1)} copy(bf16[5,128,2880]{1,2,0:T(8,128)(2,1)} %collective-permute-done.2) | data formatting | bytes 7372800 | tf_op jit(solution)/shard_map/ppermute | solution.py:239
  338.0 10.0 %fusion = f32[640,1536]{1,0:T(8,128)S(1)} fusion(bf16[640,2880]{1,0:T(8,128)(2,1)} %bitcast.108, bf16[1,2880,1536]{2,1,0:T(8,128)(2,1)} %param.22), kind=kOutput, calls=%fused_computation.6 | convolution fusion | flops 5662310400 | bytes 16465920 | tf_op jit(solution)/shard_map/dot_general | solution.py:242
  348.0 6.1 %convolution_convert_fusion = bf16[640,2880]{0,1:T(8,128)(2,1)S(1)} fusion(bf16[1,768,2880]{1,2,0:T(8,128)(2,1)} %param.23, f32[640,1536]{1,0:T(8,128)S(1)} %fusion), kind=kOutput, calls=%fused_computation.11 | convolution fusion | flops 2836930560 | bytes 12042240 | tf_op jit(solution)/shard_map/dot_general | solution.py:244
  355.4 6.2 %fusion.2 = f32[640,1536]{1,0:T(8,128)S(1)} fusion(bf16[640,2880]{1,0:T(8,128)(2,1)S(1)} %bitcast.109, bf16[1,2880,1536]{2,1,0:T(8,128)(2,1)S(1)} %bitcast.129), kind=kOutput, calls=%fused_computation.8 | convolution fusion | flops 5662310400 | bytes 16465920 | tf_op jit(solution)/shard_map/dot_general | solution.py:242
  361.7 6.9 %add_convert_fusion = bf16[640,2880]{0,1:T(8,128)(2,1)} fusion(bf16[640,2880]{0,1:T(8,128)(2,1)} %collective-permute-done.3, bf16[1,768,2880]{1,2,0:T(8,128)(2,1)S(1)} %bitcast.131, f32[640,1536]{1,0:T(8,128)S(1)} %fusion.2), kind=kOutput, calls=%fused_computation.10 | convolution fusion | flops 2844303360 | bytes 15728640 | tf_op jit(solution)/shard_map/dot_general | solution.py:244
  368.5 6.2 %copy.145 = bf16[640,2880]{1,0:T(8,128)(2,1)} copy(bf16[640,2880]{0,1:T(8,128)(2,1)} %add_convert_fusion) | data formatting | bytes 7372800 | tf_op jit(solution)/shard_map/convert_element_type | solution.py:249
  374.7 6.8 %copy.146 = bf16[5,128,2880]{2,0,1:T(8,128)(2,1)} copy(bf16[5,128,2880]{2,1,0:T(8,128)(2,1)} %bitcast.105) | data formatting | bytes 7372800 | tf_op jit(solution)/shard_map/reshape | solution.py:251
  381.5 5.3 %all-to-all-start.1 = ((bf16[5,128,2880]{2,0,1:T(8,128)(2,1)}), bf16[5,128,2880]{2,0,1:T(8,128)(2,1)}, u32[]{:S(2)}, u32[]{:S(2)}) async-start(bf16[5,128,2880]{2,0,1:T(8,128)(2,1)} %copy.146), calls=%async_computation.1 | async-start | bytes 12058624 | tf_op jit(solution)/shard_map/all_to_all | solution.py:250
  387.9 72.6 %all-to-all-done.1 = bf16[5,128,2880]{2,0,1:T(8,128)(2,1)} async-done(((bf16[5,128,2880]{2,0,1:T(8,128)(2,1)}), bf16[5,128,2880]{2,0,1:T(8,128)(2,1)}, u32[]{:S(2)}, u32[]{:S(2)}) %all-to-all-start.1) | async-done | bytes 3686432 | tf_op jit(solution)/shard_map/all_to_all | solution.py:250
  460.5 5.1 %copy.147 = bf16[5,128,2880]{2,1,0:T(8,128)(2,1)} copy(bf16[5,128,2880]{2,0,1:T(8,128)(2,1)} %all-to-all-done.1) | data formatting | bytes 7372800 | tf_op jit(solution)/shard_map/all_to_all | solution.py:250
  465.6 4.4 gather_fusion.1
  470.4 4.4 gather_fusion.2
  475.9 4.4 gather_fusion.3
  481.5 4.4 gather_fusion.4
  487.0 3.1 fusion.29
  (108 shorter events, 17.9 us)
Async XLA Ops:
  7.2 2.3 copy-start
  7.2 3.6 copy-start.9
  7.2 5.4 %copy-start.4 = (bf16[1,128,2048]{2,1,0:T(8,128)(2,1)S(1)}, bf16[1,128,2048]{2,1,0:T(8,128)(2,1)}, u32[]{:S(2)}) copy-start(bf16[1,128,2048]{2,1,0:T(8,128)(2,1)} %param.13) | copy-start | bytes 1572868
  7.2 96.1 %all-gather.6.cloned.1.call-start = ((), (), s32[]{:S(2)}) async-start(), calls=%async_computation.3 | async-start | bytes 13369344 | tf_op jit(solution)/shard_map/all_gather | solution.py:190
  9.4 159.7 %all-gather.4.cloned.1.call-start = ((), (), s32[]{:S(2)}) async-start(), calls=%async_computation.2 | async-start | bytes 6406144 | tf_op jit(solution)/shard_map/all_gather | solution.py:197
  12.9 3.7 copy-start.8
  135.4 32.2 %copy-start.7 = (s32[1,128,4]{1,2,0:T(4,128)S(1)}, s32[1,128,4]{1,2,0:T(4,128)}, u32[]{:S(2)}) copy-start(s32[1,128,4]{1,2,0:T(4,128)} %param.21) | copy-start | bytes 6148
  138.5 30.7 %collective-permute-start = (bf16[128,1024]{0,1:T(8,128)(2,1)S(1)}, bf16[128,1024]{0,1:T(8,128)(2,1)S(1)}, u32[]{:S(2)}, u32[]{:S(2)}) collective-permute-start(bf16[128,1024]{0,1:T(8,128)(2,1)S(1)} %bitcast.116), channel_id=1, source_target_pairs={{0,1},{1,0},{2,3},{3,2},{4,5},{5,4},{6,7},{7,6},{8,9},{9,8},{10,11... | collective-permute-start | bytes 786440 | tf_op jit(solution)/shard_map/ppermute | solution.py:203
  174.4 1.6 copy-start.3
  176.0 6.8 %copy-start.6 = (f32[2880]{0:T(1024)S(1)}, f32[2880]{0:T(1024)}, u32[]{:S(2)}) copy-start(f32[2880]{0:T(1024)} %param.19) | copy-start | bytes 34564
  177.2 3.6 collective-permute-start.1
  182.8 304.2 %copy-start.2 = (bf16[128,2880]{0,1:T(8,128)(2,1)}, bf16[128,2880]{0,1:T(8,128)(2,1)S(1)}, u32[]{:S(2)}) copy-start(bf16[128,2880]{0,1:T(8,128)(2,1)S(1)} %get-tuple-element.7) | copy-start | bytes 2211844
  323.9 7.8 %collective-permute-start.2 = (bf16[5,128,2880]{1,2,0:T(8,128)(2,1)}, bf16[5,128,2880]{1,2,0:T(8,128)(2,1)}, u32[]{:S(2)}, u32[]{:S(2)}) collective-permute-start(bf16[5,128,2880]{1,2,0:T(8,128)(2,1)} %copy.143), channel_id=1, source_target_pairs={{0,1},{1,0},{2,3},{3,2},{4,5},{5,4},{6,7},{7,6},{8,9},{9,8},{10,11... | collective-permute-start | bytes 11059208 | tf_op jit(solution)/shard_map/ppermute | solution.py:239
  331.7 23.1 %slice-start = ((s8[6029312]{0:T(1024)(128)(4,1)}), s8[1835008]{0:T(1024)(128)(4,1)S(1)}, s32[]{:S(2)}) async-start(s8[6029312]{0:T(1024)(128)(4,1)} %bitcast.102), calls=%async_computation.4 | async-start | bytes 3670016
  338.0 16.8 %slice-start.1 = ((s8[6029312]{0:T(1024)(128)(4,1)}), s8[4194304]{0:T(1024)(128)(4,1)S(1)}, s32[]{:S(2)}) async-start(s8[6029312]{0:T(1024)(128)(4,1)} %bitcast.102), calls=%async_computation.5 | async-start | bytes 8388608
  338.0 17.4 %slice-start.2 = ((s8[8847360]{0:T(1024)(128)(4,1)}), s8[4194304]{0:T(1024)(128)(4,1)S(1)}, s32[]{:S(2)}) async-start(s8[8847360]{0:T(1024)(128)(4,1)} %bitcast.128), calls=%async_computation.6 | async-start | bytes 8388608
  338.0 17.4 %slice-start.3 = ((s8[8847360]{0:T(1024)(128)(4,1)}), s8[4194304]{0:T(1024)(128)(4,1)S(1)}, s32[]{:S(2)}) async-start(s8[8847360]{0:T(1024)(128)(4,1)} %bitcast.128), calls=%async_computation.7 | async-start | bytes 8388608
  348.0 7.4 %slice-start.4 = ((s8[8847360]{0:T(1024)(128)(4,1)}), s8[458752]{0:T(1024)(128)(4,1)S(1)}, s32[]{:S(2)}) async-start(s8[8847360]{0:T(1024)(128)(4,1)} %bitcast.128), calls=%async_computation.8 | async-start | bytes 917504
  354.1 7.5 %collective-permute-start.3 = (bf16[640,2880]{0,1:T(8,128)(2,1)S(1)}, bf16[640,2880]{0,1:T(8,128)(2,1)}, u32[]{:S(2)}, u32[]{:S(2)}) collective-permute-start(bf16[640,2880]{0,1:T(8,128)(2,1)S(1)} %convolution_convert_fusion), channel_id=1, source_target_pairs={{0,1},{1,0},{2,3},{3,2},{4,5},{5,4},{6,7},{7,6},{8,9},{9,8},{10,11... | collective-permute-start | bytes 11059208 | tf_op jit(solution)/shard_map/ppermute | solution.py:248
  354.8 6.8 %slice-start.5 = ((s8[4423680]{0:T(1024)(128)(4,1)}), s8[4194304]{0:T(1024)(128)(4,1)S(1)}, s32[]{:S(2)}) async-start(s8[4423680]{0:T(1024)(128)(4,1)} %bitcast.130), calls=%async_computation.9 | async-start | bytes 8388608
  355.4 6.3 %slice-start.6 = ((s8[4423680]{0:T(1024)(128)(4,1)}), s8[229376]{0:T(1024)(128)(4,1)S(1)}, s32[]{:S(2)}) async-start(s8[4423680]{0:T(1024)(128)(4,1)} %bitcast.130), calls=%async_computation.10 | async-start | bytes 458752
  381.5 6.0 %copy-start.5 = (bf16[2880,64]{0,1:T(8,128)(2,1)S(1)}, bf16[2880,64]{0,1:T(8,128)(2,1)}, u32[]{:S(2)}) copy-start(bf16[2880,64]{0,1:T(8,128)(2,1)} %param.20) | copy-start | bytes 1105924
  381.5 79.0 %all-to-all-start.1 = ((bf16[5,128,2880]{2,0,1:T(8,128)(2,1)}), bf16[5,128,2880]{2,0,1:T(8,128)(2,1)}, u32[]{:S(2)}, u32[]{:S(2)}) async-start(bf16[5,128,2880]{2,0,1:T(8,128)(2,1)} %copy.146), calls=%async_computation.1 | async-start | bytes 12058624 | tf_op jit(solution)/shard_map/all_to_all | solution.py:250
  481.5 8.7 %copy-start.1 = (bf16[128,2880]{0,1:T(8,128)(2,1)S(1)}, bf16[128,2880]{0,1:T(8,128)(2,1)}, u32[]{:S(2)}) copy-start(bf16[128,2880]{0,1:T(8,128)(2,1)} %param.18) | copy-start | bytes 2211844
Sparse Core Ops, SparseCore 0:
  10.2 93.0 all-gather.5
  105.4 59.6 all-gather.3
where the time goes:
time: 506 us; the launch traced here: 497 us
  waiting for transfers between devices  162 us (32%)
  blocking collectives  124 us (25%)
  local copies, waits for them, and re-layouts  81.5 us (16%)
  starting transfers between devices  36.9 us (7%)
  matrix products  34.7 us (7%)
  Pallas kernels  32.1 us (6%)
  between operations  16 us (3%)
  other arithmetic  10.8 us (2%)
    all_to_all x1, blocking collectives, body(): lax.all_to_all(split, ('ctx', 'grp'), split_axis=1, concat_axis=1, tiled=...  124 us
    all_gather x1, waiting for transfers between devices, body(): kv_all = lax.all_gather(local_kv, 'ctx', axis=0, tiled=False)  82.7 us
    all_to_all x1, waiting for transfers between devices, body(): lax.all_to_all(summed.reshape(half_cap, owners, width), ('ctx', 'grp'), s...  72.6 us
    pallas_call x1, Pallas kernels, flash_pairs(): pl.pallas_call(kernel, grid_spec=grid_spec, out_shape=jax.ShapeDtypeStruc...  32.1 us
    ppermute x1, starting transfers between devices, body(): partner_cols = lax.ppermute(theirs_cols, 'grp', pair_perm)  29.2 us
    gather x8, local copies, waits for them, and re-layouts, body(): expert_rows[pair_dest[:, k]].astype(jnp.float32) * route_weights[:, k:k + 1]  21.4 us
    dot_general x2, matrix products, expert_half(): jnp.dot(rows.reshape(-1, width), in_weights, preferred_element_type=jnp.f...  16.2 us
    dot_general x2, matrix products, expert_half(): jnp.dot(hidden, out_weights, preferred_element_type=jnp.float32)  13 us
  transfers between devices with their start and end apart: 7, of which 4 were waited for; matrix products, arithmetic and copies ran while one was open for 5% of the time, Pallas kernels for 6%

commit v1 on v0

--- a/solution.py
+++ b/solution.py
@@ -13,20 +13,21 @@
 CACHE_TK = 256
 
 
-def flash_pairs(qpad, qpos, qstart, sink_rows, kv_all, cache_rows, bounds, scale):
+def flash_all(qpad, qpos, qstart, sink_rows, kv_all, cache_rows, bounds, steps, scale):
     pairs, rows, lanes = qpad.shape
+    tokens = qpos.shape[0]
     sources, span, width = kv_all.shape
     stretch_rows = span - cache_rows
     cache_steps = cache_rows // CACHE_TK
     n_cache = sources * cache_steps
-    n_blocks = n_cache + sources
-    v_off = width // lanes // 2
+    v_base = width // 2
+    reps = rows // tokens
 
     def block_of(j, s):
         return jnp.minimum(s[0] + j, s[1])
 
-    def kernel(s_ref, q_ref, qpos_ref, qstart_ref, sink_ref, ck_ref, cv_ref, sk_ref, sv_ref, o_ref, m_sc, l_sc, acc_sc):
-        j = pl.program_id(1)
+    def kernel(s_ref, q_ref, qpos_ref, qstart_ref, sink_ref, c_ref, t_ref, o_ref, m_sc, l_sc, acc_sc):
+        j = pl.program_id(0)
         b = s_ref[0] + j
 
         @pl.when(j == 0)
@@ -35,112 +36,143 @@
             l_sc[...] = jnp.zeros_like(l_sc)
             acc_sc[...] = jnp.zeros_like(acc_sc)
 
-        def step(k_ref, v_ref, first, count):
-            s = lax.dot_general(
-                q_ref[...], k_ref[...], (((1,), (1,)), ((), ())), preferred_element_type=jnp.float32
-            ) * scale
-            kpos = first + lax.broadcasted_iota(jnp.int32, (1, count), 1)
-            allowed = (kpos <= qpos_ref[...]) & (kpos >= qstart_ref[...])
-            m_prev = m_sc[...]
-            m_new = jnp.maximum(m_prev, jnp.max(jnp.where(allowed, s, -jnp.inf), axis=1, keepdims=True))
-            p = jnp.where(allowed, jnp.exp(s - m_new), 0.0)
-            shrink = jnp.exp(m_prev - m_new)
-            l_sc[...] = l_sc[...] * shrink + jnp.sum(p, axis=1, keepdims=True)
-            acc_sc[...] = acc_sc[...] * shrink + jnp.dot(
-                p.astype(jnp.bfloat16), v_ref[...], preferred_element_type=jnp.float32
-            )
-            m_sc[...] = m_new
+        def step(kv_ref, first, count, masked):
+            if masked:
+                kpos = first + lax.broadcasted_iota(jnp.int32, (1, count), 1)
+                allowed = ((kpos <= qpos_ref[...]) & (kpos >= qstart_ref[...]))[None]
+            for p in range(pairs):
+                keys = kv_ref[:, p * lanes:(p + 1) * lanes]
+                values = kv_ref[:, v_base + p * lanes:v_base + (p + 1) * lanes]
+                s = lax.dot_general(
+                    q_ref[p], keys, (((1,), (1,)), ((), ())), preferred_element_type=jnp.float32
+                ) * scale
+                m_prev = m_sc[p]
+                if masked:
+                    s3 = s.reshape(reps, tokens, count)
+                    top = jnp.max(jnp.where(allowed, s3, -jnp.inf), axis=2, keepdims=True).reshape(rows, 1)
+                    m_new = jnp.maximum(m_prev, top)
+                    e3 = jnp.exp(s3 - m_new.reshape(reps, tokens, 1))
+                    w = jnp.where(allowed, e3, 0.0).reshape(rows, count)
+                else:
+                    m_new = jnp.maximum(m_prev, jnp.max(s, axis=1, keepdims=True))
+                    w = jnp.exp(s - m_new)
+                shrink = jnp.exp(m_prev - m_new)
+                l_sc[p] = l_sc[p] * shrink + jnp.sum(w, axis=1, keepdims=True)
+                acc_sc[p] = acc_sc[p] * shrink + jnp.dot(
+                    w.astype(jnp.bfloat16), values, preferred_element_type=jnp.float32
+                )
+                m_sc[p] = m_new
 
         live = b <= s_ref[1]
+
+        def branch(kv_ref, first, count):
+            inside = (first >= s_ref[3]) & (first + count - 1 <= s_ref[2])
+
+            @pl.when(inside)
+            def _():
+                step(kv_ref, first, count, False)
+
+            @pl.when(jnp.logical_not(inside))
+            def _():
+                step(kv_ref, first, count, True)
 
         @pl.when(live & (b < n_cache))
         def _():
-            step(ck_ref, cv_ref, b * CACHE_TK, CACHE_TK)
+            branch(c_ref, b * CACHE_TK, CACHE_TK)
 
         @pl.when(live & (b >= n_cache))
         def _():
-            step(sk_ref, sv_ref, sources * cache_rows + (b - n_cache) * stretch_rows, stretch_rows)
-
-        @pl.when(j == pl.num_programs(1) - 1)
+            branch(t_ref, sources * cache_rows + (b - n_cache) * stretch_rows, stretch_rows)
+
+        @pl.when(j == pl.num_programs(0) - 1)
         def _():
             denom = l_sc[...] + jnp.exp(sink_ref[...] - m_sc[...])
             o_ref[...] = (acc_sc[...] / denom).astype(o_ref.dtype)
 
-    def cache_at(j, s):
+    def cache_map(j, s):
         c = jnp.minimum(block_of(j, s), n_cache - 1)
-        return c // cache_steps, c % cache_steps
-
-    def cache_k(p, j, s):
-        src, part = cache_at(j, s)
-        return (src, part, p)
-
-    def cache_v(p, j, s):
-        src, part = cache_at(j, s)
-        return (src, part, v_off + p)
-
-    def stretch_k(p, j, s):
-        return (jnp.maximum(block_of(j, s) - n_cache, 0), cache_rows // stretch_rows, p)
-
-    def stretch_v(p, j, s):
-        return (jnp.maximum(block_of(j, s) - n_cache, 0), cache_rows // stretch_rows, v_off + p)
+        return (c // cache_steps, c % cache_steps, 0)
+
+    def stretch_map(j, s):
+        return (jnp.maximum(block_of(j, s) - n_cache, 0), cache_rows // stretch_rows, 0)
 
     grid_spec = pltpu.PrefetchScalarGridSpec(
         num_scalar_prefetch=1,
-        grid=(pairs, n_blocks),
+        grid=(steps,),
         in_specs=[
-            pl.BlockSpec((None, rows, lanes), lambda p, j, s: (p, 0, 0)),
-            pl.BlockSpec((rows, 1), lambda p, j, s: (0, 0)),
-            pl.BlockSpec((rows, 1), lambda p, j, s: (0, 0)),
-            pl.BlockSpec((None, rows, 1), lambda p, j, s: (p, 0, 0)),
-            pl.BlockSpec((None, CACHE_TK, lanes), cache_k),
-            pl.BlockSpec((None, CACHE_TK, lanes), cache_v),
-            pl.BlockSpec((None, stretch_rows, lanes), stretch_k),
-            pl.BlockSpec((None, stretch_rows, lanes), stretch_v),
+            pl.BlockSpec((pairs, rows, lanes), lambda j, s: (0, 0, 0)),
+            pl.BlockSpec((tokens, 1), lambda j, s: (0, 0)),
+            pl.BlockSpec((tokens, 1), lambda j, s: (0, 0)),
+            pl.BlockSpec((pairs, rows, 1), lambda j, s: (0, 0, 0)),
+            pl.BlockSpec((None, CACHE_TK, width), cache_map),
+            pl.BlockSpec((None, stretch_rows, width), stretch_map),
         ],
-        out_specs=pl.BlockSpec((None, rows, lanes), lambda p, j, s: (p, 0, 0)),
+        out_specs=pl.BlockSpec((pairs, rows, lanes), lambda j, s: (0, 0, 0)),
         scratch_shapes=[
-            pltpu.VMEM((rows, 1), jnp.float32),
-            pltpu.VMEM((rows, 1), jnp.float32),
-            pltpu.VMEM((rows, lanes), jnp.float32),
+            pltpu.VMEM((pairs, rows, 1), jnp.float32),
+            pltpu.VMEM((pairs, rows, 1), jnp.float32),
+            pltpu.VMEM((pairs, rows, lanes), jnp.float32),
         ],
     )
-    keys = sources * span
+    keys = sources * span // 2
     return pl.pallas_call(
         kernel,
         grid_spec=grid_spec,
         out_shape=jax.ShapeDtypeStruct((pairs, rows, lanes), jnp.bfloat16),
-        compiler_params=pltpu.CompilerParams(dimension_semantics=("arbitrary", "arbitrary")),
+        compiler_params=pltpu.CompilerParams(
+            dimension_semantics=("arbitrary",), vmem_limit_bytes=48 * 1024 * 1024
+        ),
         cost_estimate=pl.CostEstimate(
-            flops=2 * pairs * rows * lanes * keys,
-            transcendentals=pairs * rows * keys // 2,
-            bytes_accessed=2 * kv_all.size + 4 * qpad.size,
+            flops=4 * pairs * rows * lanes * keys,
+            transcendentals=pairs * rows * keys,
+            bytes_accessed=kv_all.size + 4 * qpad.size,
         ),
-    )(bounds, qpad, qpos, qstart, sink_rows, kv_all, kv_all, kv_all, kv_all)
-
-
-def attention(queries_local, kv_all, cache_rows, sinks, query_pos, query_start):
+    )(bounds, qpad, qpos, qstart, sink_rows, kv_all, kv_all)
+
+
+def block_index(position, sources, cache_rows, stretch_rows):
+    cache_end = sources * cache_rows
+    return jnp.where(
+        position < cache_end,
+        position // CACHE_TK,
+        sources * (cache_rows // CACHE_TK) + (position - cache_end) // stretch_rows,
+    )
+
+
+def attention(queries_local, kv_all, cache_rows, sinks, query_pos, query_start, longest):
     tokens = queries_local.shape[0]
     groups = HEADS // KVH
     pairs = KVH // 2
     sources, span, _ = kv_all.shape
+    stretch_rows = span - cache_rows
     q6 = queries_local.reshape(tokens, pairs, 2, groups, HD).transpose(1, 2, 3, 0, 4)
     zeros = jnp.zeros_like(q6[:, 0])
     qpad = jnp.stack(
         [jnp.concatenate([q6[:, 0], zeros], axis=-1), jnp.concatenate([zeros, q6[:, 1]], axis=-1)], axis=1
     ).reshape(pairs, 2 * groups * tokens, 2 * HD)
     rows = 2 * groups * tokens
-    qpos = jnp.tile(query_pos, 2 * groups).reshape(rows, 1)
-    qstart = jnp.tile(query_start, 2 * groups).reshape(rows, 1)
     sink_rows = jnp.repeat(sinks.reshape(pairs, 2 * groups), tokens, axis=1).reshape(pairs, rows, 1)
+    first = block_index(query_start[0], sources, cache_rows, stretch_rows)
+    last = block_index(query_pos[-1], sources, cache_rows, stretch_rows)
+    bounds = jnp.stack([first, last, query_pos[0], query_start[-1]]).astype(jnp.int32)
     cache_end = sources * cache_rows
-    stretch_rows = span - cache_rows
-    low = query_start[0]
-    first = jnp.where(
-        low < cache_end, low // CACHE_TK, sources * (cache_rows // CACHE_TK) + (low - cache_end) // stretch_rows
-    )
-    last = sources * (cache_rows // CACHE_TK) + (query_pos[-1] - cache_end) // stretch_rows
-    bounds = jnp.stack([first, last]).astype(jnp.int32)
-    out = flash_pairs(qpad, qpos, qstart, sink_rows, kv_all, cache_rows, bounds, 1.0 / math.sqrt(HD))
+
+    def static_block(position):
+        if position < cache_end:
+            return position // CACHE_TK
+        return sources * (cache_rows // CACHE_TK) + (position - cache_end) // stretch_rows
+
+    steps = 1
+    for device in range(sources):
+        low_q = cache_end + device * tokens
+        high_q = low_q + tokens - 1
+        low = max(0, low_q - longest + 1)
+        blocks = static_block(high_q) - static_block(low) + 1
+        steps = max(steps, blocks)
+    out = flash_all(
+        qpad, query_pos.reshape(tokens, 1), query_start.reshape(tokens, 1), sink_rows, kv_all, cache_rows,
+        bounds, steps, 1.0 / math.sqrt(HD),
+    )
     o6 = out.reshape(pairs, 2, groups, tokens, 2, HD)
     picked = jnp.stack([o6[:, 0, :, :, 0], o6[:, 1, :, :, 1]], axis=1)
     return picked.transpose(3, 0, 1, 2, 4).reshape(tokens, HEADS * HD)
@@ -188,7 +220,7 @@
     ).astype(jnp.int32)
     local_kv = jnp.concatenate([cache_kv[0], stretch_kv[0]], axis=0)
     kv_all = lax.all_gather(local_kv, "ctx", axis=0, tiled=False)
-    attended = attention(queries[0], kv_all, cache_rows, sinks, query_pos, query_start)
+    attended = attention(queries[0], kv_all, cache_rows, sinks, query_pos, query_start, span * ctx_count // 2)
     grp_here = lax.axis_index("grp")
     parity = grp_here % 2
     grp_count = lax.axis_size("grp")

time: 506 us -> 470 us (0.929)
  waiting for transfers between devices: 162 us -> 199 us
  starting transfers between devices: 36.9 us -> 8.37 us
  blocking collectives: 124 us -> 96.8 us
  Pallas kernels: 32.1 us -> 16.3 us
  between operations: 16 us -> 22.2 us
    all_gather x1, waiting for transfers between devices: 0.01 us -> 40.6 us  [body(): lax.all_gather(lax.dynamic_slice_in_dim(out_proj, parity * head_rows, hea...]
    ppermute x1, starting transfers between devices: 29.2 us -> 0.09 us  [body(): partner_cols = lax.ppermute(theirs_cols, 'grp', pair_perm)]
    all_to_all x1, blocking collectives: 124 us -> 96.8 us  [body(): lax.all_to_all(split, ('ctx', 'grp'), split_axis=1, concat_axis=1, tiled=...]
    pallas_call x1, Pallas kernels: 32.1 us -> 16.3 us  [flash_all(): pl.pallas_call(kernel, grid_spec=grid_spec, out_shape=jax.ShapeDtypeStruc...]
  transfers between devices with their start and end apart: 7 -> 7, of which waited for: 4 -> 4; matrix products, arithmetic and copies ran while one was open for 5% -> 5% of each run, Pallas kernels for 6% -> 4%
where the time goes in v1:
time: 470 us; the launch traced here: 466 us
  waiting for transfers between devices  199 us (42%)
  blocking collectives  96.8 us (21%)
  local copies, waits for them, and re-layouts  77.4 us (16%)
  matrix products  34.7 us (7%)
  between operations  22.2 us (5%)
  Pallas kernels  16.3 us (3%)
  other arithmetic  11.5 us (2%)
  starting transfers between devices  8.37 us (2%)
    all_to_all x1, blocking collectives, body(): lax.all_to_all(split, ('ctx', 'grp'), split_axis=1, concat_axis=1, tiled=...  96.8 us
    all_gather x1, waiting for transfers between devices, body(): kv_all = lax.all_gather(local_kv, 'ctx', axis=0, tiled=False)  79.3 us
    all_to_all x1, waiting for transfers between devices, body(): lax.all_to_all(summed.reshape(half_cap, owners, width), ('ctx', 'grp'), s...  72.6 us
    all_gather x1, waiting for transfers between devices, body(): lax.all_gather(lax.dynamic_slice_in_dim(out_proj, parity * head_rows, hea...  40.6 us
    gather x8, local copies, waits for them, and re-layouts, body(): expert_rows[pair_dest[:, k]].astype(jnp.float32) * route_weights[:, k:k + 1]  21.3 us
    pallas_call x1, Pallas kernels, flash_all(): pl.pallas_call(kernel, grid_spec=grid_spec, out_shape=jax.ShapeDtypeStruc...  16.3 us
    dot_general x2, matrix products, expert_half(): jnp.dot(rows.reshape(-1, width), in_weights, preferred_element_type=jnp.f...  16.2 us
    dot_general x2, matrix products, expert_half(): jnp.dot(hidden, out_weights, preferred_element_type=jnp.float32)  13 us
  transfers between devices with their start and end apart: 7, of which 4 were waited for; matrix products, arithmetic and copies ran while one was open for 5% of the time, Pallas kernels for 4%

profile of v1, /device:TPU:1, one launch (start us, length us, event | category | flops | bytes accessed | tf_op | source)
XLA Modules:
  0.0 466.3 jit_solution(14348731074623625450)
XLA Ops:
  7.2 2.1 pad_maximum_fusion.1
  20.7 2.0 reshape_reshape.8.sink_ref
  22.7 1.3 pad_add_fusion.s_ref
  24.0 79.3 %all-gather.6.cloned.1.call-done = bf16[6144,1024]{1,0:T(8,128)(2,1)} async-done(((bf16[384,1024]{1,0:T(8,128)(2,1)}), bf16[6144,1024]{1,0:T(8,128)(2,1)}) %all-gather.6.cloned.1.call-update) | async-done | bytes 12582928 | tf_op jit(solution)/shard_map/all_gather | solution.py:222
  103.3 16.3 %shard_map.131 = bf16[4,1024,128]{2,1,0:T(8,128)(2,1)S(1)} custom-call(s32[4]{0:T(128)S(1)} %pad_add_fusion.s_ref, bf16[4,1024,128]{2,1,0:T(8,128)(2,1)S(1)} %bitcast.92, s32[128,1]{1,0:T(8,128)S(1)} %iota_add_fusion.qpos_ref, s32[128,1]{1,0:T(8,128)S(1)} %copy.125.qstart_ref, f32[4,1024,1]{2,1,0:T(8,128)S(1)} %reshape_reshape.8.sink_ref, ...), custom_call_target="tpu_custom_call" | custom-call | flops 6442450944 | bytes 8388608 | tf_op jit(solution)/shard_map/pallas_call | solution.py:118
  120.6 1.5 copy.127
  125.2 40.6 %all-gather.4.cloned.1.call-done = bf16[1024,2880]{1,0:T(8,128)(2,1)} async-done(((bf16[64,2880]{1,0:T(8,128)(2,1)}), bf16[1024,2880]{1,0:T(8,128)(2,1)}) %all-gather.4.cloned.1.call-update) | async-done | bytes 5898256 | tf_op jit(solution)/shard_map/all_gather | solution.py:229
  165.7 5.3 %fusion.30 = f32[256,2880]{0,1:T(8,128)S(1)} fusion(bf16[1024,2880]{1,0:T(8,128)(2,1)} %all-gather.4.cloned.1.call-done, bf16[128,1024]{0,1:T(8,128)(2,1)S(1)} %collective-permute-done, bf16[128,1024]{0,1:T(8,128)(2,1)S(1)} %bitcast.111), kind=kOutput, calls=%fused_computation.44 | convolution fusion | flops 1510998016 | bytes 9371648 | tf_op jit(solution)/shard_map/dot_general | solution.py:236
  171.0 1.6 copy-done.4
  174.2 2.4 scatter_custom_fusion
  176.7 2.0 fusion.14
  179.5 4.6 gather_fusion
  184.1 4.2 copy.137
  188.3 96.8 %all_to_all.10 = bf16[5,128,2880]{2,0,1:T(8,128)(2,1)} all-to-all(bf16[5,128,2880]{2,0,1:T(8,128)(2,1)S(1)} %copy.137), channel_id=1, replica_groups=mesh['ctx'=16,'grp'=8] {'ctx','grp'}, dimensions={1} | all-to-all | bytes 7372800 | tf_op jit(solution)/shard_map/all_to_all | solution.py:270
  285.2 7.9 %copy.139 = bf16[5,128,2880]{1,2,0:T(8,128)(2,1)} copy(bf16[5,128,2880]{2,0,1:T(8,128)(2,1)} %all_to_all.10) | data formatting | bytes 7372800 | tf_op jit(solution)/shard_map/all_to_all | solution.py:270
  293.0 1.6 collective-permute-start.2
  294.7 6.4 %collective-permute-done.2 = bf16[5,128,2880]{1,2,0:T(8,128)(2,1)} collective-permute-done((bf16[5,128,2880]{1,2,0:T(8,128)(2,1)}, bf16[5,128,2880]{1,2,0:T(8,128)(2,1)}, u32[]{:S(2)}, u32[]{:S(2)}) %collective-permute-start.2) | collective-permute-done | bytes 3686432 | tf_op jit(solution)/shard_map/ppermute | solution.py:271
  301.1 6.2 %copy.140 = bf16[5,128,2880]{2,1,0:T(8,128)(2,1)} copy(bf16[5,128,2880]{1,2,0:T(8,128)(2,1)} %collective-permute-done.2) | data formatting | bytes 7372800 | tf_op jit(solution)/shard_map/ppermute | solution.py:271
  307.3 10.0 %fusion = f32[640,1536]{1,0:T(8,128)S(1)} fusion(bf16[640,2880]{1,0:T(8,128)(2,1)} %bitcast.104, bf16[1,2880,1536]{2,1,0:T(8,128)(2,1)} %param.22), kind=kOutput, calls=%fused_computation.6 | convolution fusion | flops 5662310400 | bytes 16465920 | tf_op jit(solution)/shard_map/dot_general | solution.py:274
  317.3 6.1 %convolution_convert_fusion = bf16[640,2880]{0,1:T(8,128)(2,1)S(1)} fusion(bf16[1,768,2880]{1,2,0:T(8,128)(2,1)} %param.23, f32[640,1536]{1,0:T(8,128)S(1)} %fusion), kind=kOutput, calls=%fused_computation.11 | convolution fusion | flops 2836930560 | bytes 12042240 | tf_op jit(solution)/shard_map/dot_general | solution.py:276
  324.7 6.2 %fusion.2 = f32[640,1536]{1,0:T(8,128)S(1)} fusion(bf16[640,2880]{1,0:T(8,128)(2,1)S(1)} %bitcast.105, bf16[1,2880,1536]{2,1,0:T(8,128)(2,1)S(1)} %bitcast.118), kind=kOutput, calls=%fused_computation.8 | convolution fusion | flops 5662310400 | bytes 16465920 | tf_op jit(solution)/shard_map/dot_general | solution.py:274
  330.9 6.9 %add_convert_fusion = bf16[640,2880]{0,1:T(8,128)(2,1)} fusion(bf16[640,2880]{0,1:T(8,128)(2,1)} %collective-permute-done.3, bf16[1,768,2880]{1,2,0:T(8,128)(2,1)S(1)} %bitcast.120, f32[640,1536]{1,0:T(8,128)S(1)} %fusion.2), kind=kOutput, calls=%fused_computation.10 | convolution fusion | flops 2844303360 | bytes 15728640 | tf_op jit(solution)/shard_map/dot_general | solution.py:276
  337.8 6.2 %copy.141 = bf16[640,2880]{1,0:T(8,128)(2,1)} copy(bf16[640,2880]{0,1:T(8,128)(2,1)} %add_convert_fusion) | data formatting | bytes 7372800 | tf_op jit(solution)/shard_map/convert_element_type | solution.py:281
  344.0 6.8 %copy.142 = bf16[5,128,2880]{2,0,1:T(8,128)(2,1)} copy(bf16[5,128,2880]{2,1,0:T(8,128)(2,1)} %bitcast.102) | data formatting | bytes 7372800 | tf_op jit(solution)/shard_map/reshape | solution.py:283
  350.8 5.2 %all-to-all-start.1 = ((bf16[5,128,2880]{2,0,1:T(8,128)(2,1)}), bf16[5,128,2880]{2,0,1:T(8,128)(2,1)}, u32[]{:S(2)}, u32[]{:S(2)}) async-start(bf16[5,128,2880]{2,0,1:T(8,128)(2,1)} %copy.142), calls=%async_computation.1 | async-start | bytes 12058624 | tf_op jit(solution)/shard_map/all_to_all | solution.py:282
  357.1 72.6 %all-to-all-done.1 = bf16[5,128,2880]{2,0,1:T(8,128)(2,1)} async-done(((bf16[5,128,2880]{2,0,1:T(8,128)(2,1)}), bf16[5,128,2880]{2,0,1:T(8,128)(2,1)}, u32[]{:S(2)}, u32[]{:S(2)}) %all-to-all-start.1) | async-done | bytes 3686432 | tf_op jit(solution)/shard_map/all_to_all | solution.py:282
  429.7 5.1 %copy.143 = bf16[5,128,2880]{2,1,0:T(8,128)(2,1)} copy(bf16[5,128,2880]{2,0,1:T(8,128)(2,1)} %all-to-all-done.1) | data formatting | bytes 7372800 | tf_op jit(solution)/shard_map/all_to_all | solution.py:282
  434.8 4.4 gather_fusion.1
  439.5 4.4 gather_fusion.2
  445.1 4.4 gather_fusion.3
  450.6 4.4 gather_fusion.4
  456.2 3.1 fusion.29
  (108 shorter events, 16.2 us)
Async XLA Ops:
  7.2 2.3 copy-start
  7.2 3.6 copy-start.10
  7.2 11.9 %copy-start.5 = (bf16[1,128,2048]{2,1,0:T(8,128)(2,1)S(1)}, bf16[1,128,2048]{2,1,0:T(8,128)(2,1)}, u32[]{:S(2)}) copy-start(bf16[1,128,2048]{2,1,0:T(8,128)(2,1)} %param.13) | copy-start | bytes 1572868
  7.2 96.1 %all-gather.6.cloned.1.call-start = ((), (), s32[]{:S(2)}) async-start(), calls=%async_computation.3 | async-start | bytes 13369344 | tf_op jit(solution)/shard_map/all_gather | solution.py:222
  9.4 156.3 %all-gather.4.cloned.1.call-start = ((), (), s32[]{:S(2)}) async-start(), calls=%async_computation.2 | async-start | bytes 6406144 | tf_op jit(solution)/shard_map/all_gather | solution.py:229
  19.4 1.1 copy-start.9
  119.6 1.0 copy-start.2
  120.6 3.1 copy-start.8
  123.6 42.1 %collective-permute-start = (bf16[128,1024]{0,1:T(8,128)(2,1)S(1)}, bf16[128,1024]{0,1:T(8,128)(2,1)S(1)}, u32[]{:S(2)}, u32[]{:S(2)}) collective-permute-start(bf16[128,1024]{0,1:T(8,128)(2,1)S(1)} %bitcast.112), channel_id=1, source_target_pairs={{0,1},{1,0},{2,3},{3,2},{4,5},{5,4},{6,7},{7,6},{8,9},{9,8},{10,11... | collective-permute-start | bytes 786440 | tf_op jit(solution)/shard_map/ppermute | solution.py:235
  171.0 1.6 copy-start.4
  172.6 6.1 %copy-start.7 = (f32[2880]{0:T(1024)S(1)}, f32[2880]{0:T(1024)}, u32[]{:S(2)}) copy-start(f32[2880]{0:T(1024)} %param.19) | copy-start | bytes 34564
  172.7 4.0 collective-permute-start.1
  178.7 277.5 %copy-start.3 = (bf16[128,2880]{0,1:T(8,128)(2,1)}, bf16[128,2880]{0,1:T(8,128)(2,1)S(1)}, u32[]{:S(2)}) copy-start(bf16[128,2880]{0,1:T(8,128)(2,1)S(1)} %get-tuple-element.7) | copy-start | bytes 2211844
  293.0 8.0 %collective-permute-start.2 = (bf16[5,128,2880]{1,2,0:T(8,128)(2,1)}, bf16[5,128,2880]{1,2,0:T(8,128)(2,1)}, u32[]{:S(2)}, u32[]{:S(2)}) collective-permute-start(bf16[5,128,2880]{1,2,0:T(8,128)(2,1)} %copy.139), channel_id=1, source_target_pairs={{0,1},{1,0},{2,3},{3,2},{4,5},{5,4},{6,7},{7,6},{8,9},{9,8},{10,11... | collective-permute-start | bytes 11059208 | tf_op jit(solution)/shard_map/ppermute | solution.py:271
  301.1 23.0 %slice-start = ((s8[6029312]{0:T(1024)(128)(4,1)}), s8[1835008]{0:T(1024)(128)(4,1)S(1)}, s32[]{:S(2)}) async-start(s8[6029312]{0:T(1024)(128)(4,1)} %bitcast.97), calls=%async_computation.4 | async-start | bytes 3670016
  307.3 16.8 %slice-start.1 = ((s8[6029312]{0:T(1024)(128)(4,1)}), s8[4194304]{0:T(1024)(128)(4,1)S(1)}, s32[]{:S(2)}) async-start(s8[6029312]{0:T(1024)(128)(4,1)} %bitcast.97), calls=%async_computation.5 | async-start | bytes 8388608
  307.3 17.3 %slice-start.2 = ((s8[8847360]{0:T(1024)(128)(4,1)}), s8[4194304]{0:T(1024)(128)(4,1)S(1)}, s32[]{:S(2)}) async-start(s8[8847360]{0:T(1024)(128)(4,1)} %bitcast.117), calls=%async_computation.6 | async-start | bytes 8388608
  307.3 17.3 %slice-start.3 = ((s8[8847360]{0:T(1024)(128)(4,1)}), s8[4194304]{0:T(1024)(128)(4,1)S(1)}, s32[]{:S(2)}) async-start(s8[8847360]{0:T(1024)(128)(4,1)} %bitcast.117), calls=%async_computation.7 | async-start | bytes 8388608
  317.3 7.3 %slice-start.4 = ((s8[8847360]{0:T(1024)(128)(4,1)}), s8[458752]{0:T(1024)(128)(4,1)S(1)}, s32[]{:S(2)}) async-start(s8[8847360]{0:T(1024)(128)(4,1)} %bitcast.117), calls=%async_computation.8 | async-start | bytes 917504
  323.5 7.4 %collective-permute-start.3 = (bf16[640,2880]{0,1:T(8,128)(2,1)S(1)}, bf16[640,2880]{0,1:T(8,128)(2,1)}, u32[]{:S(2)}, u32[]{:S(2)}) collective-permute-start(bf16[640,2880]{0,1:T(8,128)(2,1)S(1)} %convolution_convert_fusion), channel_id=1, source_target_pairs={{0,1},{1,0},{2,3},{3,2},{4,5},{5,4},{6,7},{7,6},{8,9},{9,8},{10,11... | collective-permute-start | bytes 11059208 | tf_op jit(solution)/shard_map/ppermute | solution.py:280
  324.1 6.8 %slice-start.5 = ((s8[4423680]{0:T(1024)(128)(4,1)}), s8[4194304]{0:T(1024)(128)(4,1)S(1)}, s32[]{:S(2)}) async-start(s8[4423680]{0:T(1024)(128)(4,1)} %bitcast.119), calls=%async_computation.9 | async-start | bytes 8388608
  324.6 6.3 %slice-start.6 = ((s8[4423680]{0:T(1024)(128)(4,1)}), s8[229376]{0:T(1024)(128)(4,1)S(1)}, s32[]{:S(2)}) async-start(s8[4423680]{0:T(1024)(128)(4,1)} %bitcast.119), calls=%async_computation.10 | async-start | bytes 458752
  350.8 5.9 %copy-start.6 = (bf16[2880,64]{0,1:T(8,128)(2,1)S(1)}, bf16[2880,64]{0,1:T(8,128)(2,1)}, u32[]{:S(2)}) copy-start(bf16[2880,64]{0,1:T(8,128)(2,1)} %param.20) | copy-start | bytes 1105924
  350.8 78.9 %all-to-all-start.1 = ((bf16[5,128,2880]{2,0,1:T(8,128)(2,1)}), bf16[5,128,2880]{2,0,1:T(8,128)(2,1)}, u32[]{:S(2)}, u32[]{:S(2)}) async-start(bf16[5,128,2880]{2,0,1:T(8,128)(2,1)} %copy.142), calls=%async_computation.1 | async-start | bytes 12058624 | tf_op jit(solution)/shard_map/all_to_all | solution.py:282
  450.6 8.7 %copy-start.1 = (bf16[128,2880]{0,1:T(8,128)(2,1)S(1)}, bf16[128,2880]{0,1:T(8,128)(2,1)}, u32[]{:S(2)}) copy-start(bf16[128,2880]{0,1:T(8,128)(2,1)} %param.18) | copy-start | bytes 2211844
Sparse Core Ops, SparseCore 0:
  10.2 93.0 all-gather.5
  106.0 59.6 all-gather.3

commit v2 on v1

--- a/solution.py
+++ b/solution.py
@@ -226,15 +226,20 @@
     grp_count = lax.axis_size("grp")
     pair_perm = [(g, g ^ 1) for g in range(grp_count)]
     head_rows = out_proj.shape[0] // 2
-    proj_half = lax.all_gather(
-        lax.dynamic_slice_in_dim(out_proj, parity * head_rows, head_rows, 0), "ctx", axis=0, tiled=True
-    )
+    proj_local = lax.dynamic_slice_in_dim(out_proj, parity * head_rows, head_rows, 0)
+    proj_shards = [proj_local] + [
+        lax.ppermute(proj_local, "ctx", [(s, (s + d) % ctx_count) for s in range(ctx_count)])
+        for d in range(1, ctx_count)
+    ]
+    proj_half = jnp.stack(proj_shards).reshape(ctx_count * head_rows, -1)
+    shard_order = (ctx_here - jnp.arange(ctx_count, dtype=jnp.int32)) % ctx_count
     by_parity = attended.reshape(tokens, HEADS // 2, 2, HD)
     mine = jnp.where(parity == 0, by_parity[:, :, 0], by_parity[:, :, 1]).reshape(tokens, -1)
     theirs_cols = jnp.where(parity == 0, by_parity[:, :, 1], by_parity[:, :, 0]).reshape(tokens, -1)
     partner_cols = lax.ppermute(theirs_cols, "grp", pair_perm)
+    stacked = jnp.concatenate([mine, partner_cols], axis=0).reshape(2 * tokens, ctx_count, -1)
     both = jnp.dot(
-        jnp.concatenate([mine, partner_cols], axis=0), proj_half, preferred_element_type=jnp.float32
+        jnp.take(stacked, shard_order, axis=1).reshape(2 * tokens, -1), proj_half, preferred_element_type=jnp.float32
     )
     back = lax.ppermute(both[tokens:], "grp", pair_perm)
     projected = both[:tokens] + back

time: 470 us -> 565 us (1.20)
  starting transfers between devices: 8.37 us -> 41.9 us
  blocking collectives: 96.8 us -> 130 us
  local copies, waits for them, and re-layouts: 77.4 us -> 97.7 us
  Pallas kernels: 16.3 us -> 24.7 us
    ppermute x0 -> x15, waiting for transfers between devices: none -> 65.8 us  [body(): lax.ppermute(proj_local, 'ctx', [(s, (s + d) % ctx_count) for s in range(...]
    all_gather x1 -> x0, waiting for transfers between devices: 40.6 us -> none  [body(): lax.all_gather(lax.dynamic_slice_in_dim(out_proj, parity * head_rows, hea...]
    all_to_all x1, blocking collectives: 96.8 us -> 130 us  [body(): lax.all_to_all(split, ('ctx', 'grp'), split_axis=1, concat_axis=1, tiled=...]
    all_gather x1, waiting for transfers between devices: 79.3 us -> 48.7 us  [body(): kv_all = lax.all_gather(local_kv, 'ctx', axis=0, tiled=False)]
    ppermute x0 -> x15, starting transfers between devices: none -> 21 us  [body(): lax.ppermute(proj_local, 'ctx', [(s, (s + d) % ctx_count) for s in range(...]
    unnamed x39 -> x54, local copies, waits for them, and re-layouts: 4.03 us -> 21.6 us
    ppermute x1, starting transfers between devices: 0.09 us -> 13.9 us  [body(): partner_cols = lax.ppermute(theirs_cols, 'grp', pair_perm)]
    pallas_call x1, Pallas kernels: 16.3 us -> 24.7 us  [flash_all(): pl.pallas_call(kernel, grid_spec=grid_spec, out_shape=jax.ShapeDtypeStruc...]
  transfers between devices with their start and end apart: 7 -> 21, of which waited for: 4 -> 9; matrix products, arithmetic and copies ran while one was open for 5% -> 8% of each run, Pallas kernels for 4% -> 4%
where the time goes in v2:
time: 565 us; the launch traced here: 558 us
  waiting for transfers between devices  194 us (34%)
  blocking collectives  130 us (23%)
  local copies, waits for them, and re-layouts  97.7 us (17%)
  starting transfers between devices  41.9 us (7%)
  matrix products  34.7 us (6%)
  Pallas kernels  24.7 us (4%)
  between operations  22.7 us (4%)
  other arithmetic  13.6 us (2%)
    all_to_all x1, blocking collectives, body(): lax.all_to_all(split, ('ctx', 'grp'), split_axis=1, concat_axis=1, tiled=...  130 us
    all_to_all x1, waiting for transfers between devices, body(): lax.all_to_all(summed.reshape(half_cap, owners, width), ('ctx', 'grp'), s...  72.6 us
    ppermute x15, waiting for transfers between devices, body(): lax.ppermute(proj_local, 'ctx', [(s, (s + d) % ctx_count) for s in range(...  65.8 us
    all_gather x1, waiting for transfers between devices, body(): kv_all = lax.all_gather(local_kv, 'ctx', axis=0, tiled=False)  48.7 us
    pallas_call x1, Pallas kernels, flash_all(): pl.pallas_call(kernel, grid_spec=grid_spec, out_shape=jax.ShapeDtypeStruc...  24.7 us
    unnamed x54, local copies, waits for them, and re-layouts  21.6 us
    gather x8, local copies, waits for them, and re-layouts, body(): expert_rows[pair_dest[:, k]].astype(jnp.float32) * route_weights[:, k:k + 1]  21.4 us
    ppermute x15, starting transfers between devices, body(): lax.ppermute(proj_local, 'ctx', [(s, (s + d) % ctx_count) for s in range(...  21 us
  transfers between devices with their start and end apart: 21, of which 9 were waited for; matrix products, arithmetic and copies ran while one was open for 8% of the time, Pallas kernels for 4%

profile of v2, /device:TPU:1, one launch (start us, length us, event | category | flops | bytes accessed | tf_op | source)
XLA Modules:
  0.0 558.4 jit_solution(10868830934768467267)
XLA Ops:
  12.8 2.5 collective-permute-start.2
  41.7 3.2 collective-permute-start.7
  49.9 32.4 %collective-permute-done.4 = bf16[64,2880]{1,0:T(8,128)(2,1)} collective-permute-done((bf16[64,2880]{1,0:T(8,128)(2,1)}, bf16[64,2880]{1,0:T(8,128)(2,1)}, u32[]{:S(2)}, u32[]{:S(2)}) %collective-permute-start.4) | collective-permute-done | bytes 368672 | tf_op jit(solution)/shard_map/ppermute | solution.py:231
  85.9 3.8 collective-permute-start.11
  93.4 2.8 collective-permute-done.8
  97.0 8.5 %collective-permute-done.9 = bf16[64,2880]{1,0:T(8,128)(2,1)S(1)} collective-permute-done((bf16[64,2880]{1,0:T(8,128)(2,1)}, bf16[64,2880]{1,0:T(8,128)(2,1)S(1)}, u32[]{:S(2)}, u32[]{:S(2)}) %collective-permute-start.9) | collective-permute-done | bytes 368672 | tf_op jit(solution)/shard_map/ppermute | solution.py:231
  107.1 4.4 collective-permute-done.11
  112.3 15.3 %collective-permute-done.12 = bf16[64,2880]{1,0:T(8,128)(2,1)S(1)} collective-permute-done((bf16[64,2880]{1,0:T(8,128)(2,1)}, bf16[64,2880]{1,0:T(8,128)(2,1)S(1)}, u32[]{:S(2)}, u32[]{:S(2)}) %collective-permute-start.12) | collective-permute-done | bytes 368672 | tf_op jit(solution)/shard_map/ppermute | solution.py:231
  132.2 48.7 %all-gather.3.cloned.1.call-done = bf16[6144,1024]{1,0:T(8,128)(2,1)} async-done(((bf16[384,1024]{1,0:T(8,128)(2,1)}), bf16[6144,1024]{1,0:T(8,128)(2,1)}) %all-gather.3.cloned.1.call-update) | async-done | bytes 12582928 | tf_op jit(solution)/shard_map/all_gather | solution.py:222
  180.9 24.7 %shard_map.131 = bf16[4,1024,128]{2,1,0:T(8,128)(2,1)S(1)} custom-call(s32[4]{0:T(128)S(1)} %pad_add_fusion.s_ref, bf16[4,1024,128]{2,1,0:T(8,128)(2,1)S(1)} %bitcast.133, s32[128,1]{1,0:T(8,128)S(1)} %iota_add_fusion.qpos_ref, s32[128,1]{1,0:T(8,128)S(1)} %copy.128.qstart_ref, f32[4,1024,1]{2,1,0:T(8,128)S(1)} %reshape_reshape.8.sink_ref, ...), custom_call_target="tpu_custom_call" | custom-call | flops 6442450944 | bytes 8388608 | tf_op jit(solution)/shard_map/pallas_call | solution.py:118
  209.6 13.9 %collective-permute-start = (bf16[128,1024]{0,1:T(8,128)(2,1)S(1)}, bf16[128,1024]{0,1:T(8,128)(2,1)S(1)}, u32[]{:S(2)}, u32[]{:S(2)}) collective-permute-start(bf16[128,1024]{0,1:T(8,128)(2,1)S(1)} %bitcast.152), channel_id=1, source_target_pairs={{0,1},{1,0},{2,3},{3,2},{4,5},{5,4},{6,7},{7,6},{8,9},{9,8},{10,11... | collective-permute-start | bytes 786440 | tf_op jit(solution)/shard_map/ppermute | solution.py:239
  226.0 5.3 convolution_bitcast_fusion
  239.1 4.6 gather_fusion.1
  243.7 4.2 copy.140
  247.9 129.5 %all_to_all.10 = bf16[5,128,2880]{2,0,1:T(8,128)(2,1)} all-to-all(bf16[5,128,2880]{2,0,1:T(8,128)(2,1)S(1)} %copy.140), channel_id=1, replica_groups=mesh['ctx'=16,'grp'=8] {'ctx','grp'}, dimensions={1} | all-to-all | bytes 7372800 | tf_op jit(solution)/shard_map/all_to_all | solution.py:275
  377.4 7.9 %copy.142 = bf16[5,128,2880]{1,2,0:T(8,128)(2,1)} copy(bf16[5,128,2880]{2,0,1:T(8,128)(2,1)} %all_to_all.10) | data formatting | bytes 7372800 | tf_op jit(solution)/shard_map/all_to_all | solution.py:275
  386.6 6.4 %collective-permute-done.17 = bf16[5,128,2880]{1,2,0:T(8,128)(2,1)} collective-permute-done((bf16[5,128,2880]{1,2,0:T(8,128)(2,1)}, bf16[5,128,2880]{1,2,0:T(8,128)(2,1)}, u32[]{:S(2)}, u32[]{:S(2)}) %collective-permute-start.17) | collective-permute-done | bytes 3686432 | tf_op jit(solution)/shard_map/ppermute | solution.py:276
  393.0 6.6 %copy.143 = bf16[5,128,2880]{2,1,0:T(8,128)(2,1)} copy(bf16[5,128,2880]{1,2,0:T(8,128)(2,1)} %collective-permute-done.17) | data formatting | bytes 7372800 | tf_op jit(solution)/shard_map/ppermute | solution.py:276
  399.6 10.0 %fusion = f32[640,1536]{1,0:T(8,128)S(1)} fusion(bf16[640,2880]{1,0:T(8,128)(2,1)} %bitcast.145, bf16[1,2880,1536]{2,1,0:T(8,128)(2,1)} %param.22), kind=kOutput, calls=%fused_computation.7 | convolution fusion | flops 5662310400 | bytes 16465920 | tf_op jit(solution)/shard_map/dot_general | solution.py:279
  409.6 6.1 %convolution_convert_fusion = bf16[640,2880]{0,1:T(8,128)(2,1)S(1)} fusion(bf16[1,768,2880]{1,2,0:T(8,128)(2,1)} %param.23, f32[640,1536]{1,0:T(8,128)S(1)} %fusion), kind=kOutput, calls=%fused_computation.12 | convolution fusion | flops 2836930560 | bytes 12042240 | tf_op jit(solution)/shard_map/dot_general | solution.py:281
  416.8 6.2 %fusion.2 = f32[640,1536]{1,0:T(8,128)S(1)} fusion(bf16[640,2880]{1,0:T(8,128)(2,1)S(1)} %bitcast.146, bf16[1,2880,1536]{2,1,0:T(8,128)(2,1)S(1)} %bitcast.159), kind=kOutput, calls=%fused_computation.9 | convolution fusion | flops 5662310400 | bytes 16465920 | tf_op jit(solution)/shard_map/dot_general | solution.py:279
  423.0 6.9 %add_convert_fusion = bf16[640,2880]{0,1:T(8,128)(2,1)} fusion(bf16[640,2880]{0,1:T(8,128)(2,1)} %collective-permute-done.18, bf16[1,768,2880]{1,2,0:T(8,128)(2,1)S(1)} %bitcast.161, f32[640,1536]{1,0:T(8,128)S(1)} %fusion.2), kind=kOutput, calls=%fused_computation.11 | convolution fusion | flops 2844303360 | bytes 15728640 | tf_op jit(solution)/shard_map/dot_general | solution.py:281
  429.9 6.2 %copy.144 = bf16[640,2880]{1,0:T(8,128)(2,1)} copy(bf16[640,2880]{0,1:T(8,128)(2,1)} %add_convert_fusion) | data formatting | bytes 7372800 | tf_op jit(solution)/shard_map/convert_element_type | solution.py:286
  436.1 6.8 %copy.145 = bf16[5,128,2880]{2,0,1:T(8,128)(2,1)} copy(bf16[5,128,2880]{2,1,0:T(8,128)(2,1)} %bitcast.143) | data formatting | bytes 7372800 | tf_op jit(solution)/shard_map/reshape | solution.py:288
  442.9 5.2 all-to-all-start.1
  449.1 72.6 %all-to-all-done.1 = bf16[5,128,2880]{2,0,1:T(8,128)(2,1)} async-done(((bf16[5,128,2880]{2,0,1:T(8,128)(2,1)}), bf16[5,128,2880]{2,0,1:T(8,128)(2,1)}, u32[]{:S(2)}, u32[]{:S(2)}) %all-to-all-start.1) | async-done | bytes 3686432 | tf_op jit(solution)/shard_map/all_to_all | solution.py:287
  521.7 5.1 copy.146
  526.8 4.4 gather_fusion.2
  531.6 4.4 gather_fusion.3
  537.1 4.4 gather_fusion.4
  542.7 4.4 gather_fusion.5
  548.2 3.1 fusion.29
  (156 shorter events, 65.3 us)
Async XLA Ops:
  7.2 12.6 %copy-start.10 = (s32[1,8]{1,0:T(1,128)S(1)}, s32[1,8]{1,0:T(1,128)}, u32[]{:S(2)}) copy-start(s32[1,8]{1,0:T(1,128)} %param.16) | copy-start | bytes 100
  7.2 12.7 %copy-start.5 = (bf16[1,128,2048]{2,1,0:T(8,128)(2,1)S(1)}, bf16[1,128,2048]{2,1,0:T(8,128)(2,1)}, u32[]{:S(2)}) copy-start(bf16[1,128,2048]{2,1,0:T(8,128)(2,1)} %param.13) | copy-start | bytes 1572868
  7.2 13.0 %copy-start.8 = (s32[1,128,4]{1,2,0:T(4,128)S(1)}, s32[1,128,4]{1,2,0:T(4,128)}, u32[]{:S(2)}) copy-start(s32[1,128,4]{1,2,0:T(4,128)} %param.21) | copy-start | bytes 6148
  7.2 173.7 %all-gather.3.cloned.1.call-start = ((), (), s32[]{:S(2)}) async-start(), calls=%async_computation.2 | async-start | bytes 13369344 | tf_op jit(solution)/shard_map/all_gather | solution.py:222
  10.8 27.9 %collective-permute-start.1 = (bf16[64,2880]{1,0:T(8,128)(2,1)}, bf16[64,2880]{1,0:T(8,128)(2,1)}, u32[]{:S(2)}, u32[]{:S(2)}) collective-permute-start(bf16[64,2880]{1,0:T(8,128)(2,1)} %copy.155), channel_id=1, source_target_pairs={{0,8},{8,16},{16,24},{24,32},{32,40},{40,48},{48,56},{56,64},{64,7... | collective-permute-start | bytes 1105928 | tf_op jit(solution)/shard_map/ppermute | solution.py:231
  12.8 28.9 %collective-permute-start.2 = (bf16[64,2880]{1,0:T(8,128)(2,1)}, bf16[64,2880]{1,0:T(8,128)(2,1)}, u32[]{:S(2)}, u32[]{:S(2)}) collective-permute-start(bf16[64,2880]{1,0:T(8,128)(2,1)} %copy.155), channel_id=1, source_target_pairs={{0,16},{8,24},{16,32},{24,40},{32,48},{40,56},{48,64},{56,72},{64,... | collective-permute-start | bytes 1105928 | tf_op jit(solution)/shard_map/ppermute | solution.py:231
  15.2 31.4 %collective-permute-start.3 = (bf16[64,2880]{1,0:T(8,128)(2,1)}, bf16[64,2880]{1,0:T(8,128)(2,1)}, u32[]{:S(2)}, u32[]{:S(2)}) collective-permute-start(bf16[64,2880]{1,0:T(8,128)(2,1)} %copy.155), channel_id=1, source_target_pairs={{0,24},{8,32},{16,40},{24,48},{32,56},{40,64},{48,72},{56,80},{64,... | collective-permute-start | bytes 1105928 | tf_op jit(solution)/shard_map/ppermute | solution.py:231
  17.4 65.0 %collective-permute-start.4 = (bf16[64,2880]{1,0:T(8,128)(2,1)}, bf16[64,2880]{1,0:T(8,128)(2,1)}, u32[]{:S(2)}, u32[]{:S(2)}) collective-permute-start(bf16[64,2880]{1,0:T(8,128)(2,1)} %copy.155), channel_id=1, source_target_pairs={{0,32},{8,40},{16,48},{24,56},{32,64},{40,72},{48,80},{56,88},{64,... | collective-permute-start | bytes 1105928 | tf_op jit(solution)/shard_map/ppermute | solution.py:231
  18.7 65.4 %collective-permute-start.5 = (bf16[64,2880]{1,0:T(8,128)(2,1)}, bf16[64,2880]{1,0:T(8,128)(2,1)}, u32[]{:S(2)}, u32[]{:S(2)}) collective-permute-start(bf16[64,2880]{1,0:T(8,128)(2,1)} %copy.155), channel_id=1, source_target_pairs={{0,40},{8,48},{16,56},{24,64},{32,72},{40,80},{48,88},{56,96},{64,... | collective-permute-start | bytes 1105928 | tf_op jit(solution)/shard_map/ppermute | solution.py:231
  21.2 11.5 %copy-start.9 = (f32[32]{0:T(128)S(1)}, f32[32]{0:T(128)}, u32[]{:S(2)}) copy-start(f32[32]{0:T(128)} %param.17) | copy-start | bytes 388
  38.7 47.3 %collective-permute-start.6 = (bf16[64,2880]{1,0:T(8,128)(2,1)}, bf16[64,2880]{1,0:T(8,128)(2,1)S(1)}, u32[]{:S(2)}, u32[]{:S(2)}) collective-permute-start(bf16[64,2880]{1,0:T(8,128)(2,1)} %copy.155), channel_id=1, source_target_pairs={{0,48},{8,56},{16,64},{24,72},{32,80},{40,88},{48,96},{56,104},{64... | collective-permute-start | bytes 1105928 | tf_op jit(solution)/shard_map/ppermute | solution.py:231
  41.7 48.9 %collective-permute-start.7 = (bf16[64,2880]{1,0:T(8,128)(2,1)}, bf16[64,2880]{1,0:T(8,128)(2,1)S(1)}, u32[]{:S(2)}, u32[]{:S(2)}) collective-permute-start(bf16[64,2880]{1,0:T(8,128)(2,1)} %copy.155), channel_id=1, source_target_pairs={{0,56},{8,64},{16,72},{24,80},{32,88},{40,96},{48,104},{56,112},{6... | collective-permute-start | bytes 1105928 | tf_op jit(solution)/shard_map/ppermute | solution.py:231
  46.6 49.6 %collective-permute-start.8 = (bf16[64,2880]{1,0:T(8,128)(2,1)}, bf16[64,2880]{1,0:T(8,128)(2,1)S(1)}, u32[]{:S(2)}, u32[]{:S(2)}) collective-permute-start(bf16[64,2880]{1,0:T(8,128)(2,1)} %copy.155), channel_id=1, source_target_pairs={{0,64},{8,72},{16,80},{24,88},{32,96},{40,104},{48,112},{56,120},{... | collective-permute-start | bytes 1105928 | tf_op jit(solution)/shard_map/ppermute | solution.py:231
  82.4 23.1 %collective-permute-start.9 = (bf16[64,2880]{1,0:T(8,128)(2,1)}, bf16[64,2880]{1,0:T(8,128)(2,1)S(1)}, u32[]{:S(2)}, u32[]{:S(2)}) collective-permute-start(bf16[64,2880]{1,0:T(8,128)(2,1)} %copy.155), channel_id=1, source_target_pairs={{0,72},{8,80},{16,88},{24,96},{32,104},{40,112},{48,120},{56,0},{6... | collective-permute-start | bytes 1105928 | tf_op jit(solution)/shard_map/ppermute | solution.py:231
  84.1 22.2 %collective-permute-start.10 = (bf16[64,2880]{1,0:T(8,128)(2,1)}, bf16[64,2880]{1,0:T(8,128)(2,1)S(1)}, u32[]{:S(2)}, u32[]{:S(2)}) collective-permute-start(bf16[64,2880]{1,0:T(8,128)(2,1)} %copy.155), channel_id=1, source_target_pairs={{0,80},{8,88},{16,96},{24,104},{32,112},{40,120},{48,0},{56,8},{64... | collective-permute-start | bytes 1105928 | tf_op jit(solution)/shard_map/ppermute | solution.py:231
  85.9 25.6 %collective-permute-start.11 = (bf16[64,2880]{1,0:T(8,128)(2,1)}, bf16[64,2880]{1,0:T(8,128)(2,1)S(1)}, u32[]{:S(2)}, u32[]{:S(2)}) collective-permute-start(bf16[64,2880]{1,0:T(8,128)(2,1)} %copy.155), channel_id=1, source_target_pairs={{0,88},{8,96},{16,104},{24,112},{32,120},{40,0},{48,8},{56,16},{64... | collective-permute-start | bytes 1105928 | tf_op jit(solution)/shard_map/ppermute | solution.py:231
  90.5 37.1 %collective-permute-start.12 = (bf16[64,2880]{1,0:T(8,128)(2,1)}, bf16[64,2880]{1,0:T(8,128)(2,1)S(1)}, u32[]{:S(2)}, u32[]{:S(2)}) collective-permute-start(bf16[64,2880]{1,0:T(8,128)(2,1)} %copy.155), channel_id=1, source_target_pairs={{0,96},{8,104},{16,112},{24,120},{32,0},{40,8},{48,16},{56,24},{64... | collective-permute-start | bytes 1105928 | tf_op jit(solution)/shard_map/ppermute | solution.py:231
  96.2 32.2 %collective-permute-start.13 = (bf16[64,2880]{1,0:T(8,128)(2,1)}, bf16[64,2880]{1,0:T(8,128)(2,1)S(1)}, u32[]{:S(2)}, u32[]{:S(2)}) collective-permute-start(bf16[64,2880]{1,0:T(8,128)(2,1)} %copy.155), channel_id=1, source_target_pairs={{0,104},{8,112},{16,120},{24,0},{32,8},{40,16},{48,24},{56,32},{64... | collective-permute-start | bytes 1105928 | tf_op jit(solution)/shard_map/ppermute | solution.py:231
  105.5 25.9 %collective-permute-start.14 = (bf16[64,2880]{1,0:T(8,128)(2,1)}, bf16[64,2880]{1,0:T(8,128)(2,1)S(1)}, u32[]{:S(2)}, u32[]{:S(2)}) collective-permute-start(bf16[64,2880]{1,0:T(8,128)(2,1)} %copy.155), channel_id=1, source_target_pairs={{0,112},{8,120},{16,0},{24,8},{32,16},{40,24},{48,32},{56,40},{64,... | collective-permute-start | bytes 1105928 | tf_op jit(solution)/shard_map/ppermute | solution.py:231
  106.3 117.3 %collective-permute-start.15 = (bf16[64,2880]{1,0:T(8,128)(2,1)}, bf16[64,2880]{1,0:T(8,128)(2,1)}, u32[]{:S(2)}, u32[]{:S(2)}) collective-permute-start(bf16[64,2880]{1,0:T(8,128)(2,1)} %copy.155), channel_id=1, source_target_pairs={{0,120},{8,0},{16,8},{24,16},{32,24},{40,32},{48,40},{56,48},{64,5... | collective-permute-start | bytes 1105928 | tf_op jit(solution)/shard_map/ppermute | solution.py:231
  209.6 15.7 %collective-permute-start = (bf16[128,1024]{0,1:T(8,128)(2,1)S(1)}, bf16[128,1024]{0,1:T(8,128)(2,1)S(1)}, u32[]{:S(2)}, u32[]{:S(2)}) collective-permute-start(bf16[128,1024]{0,1:T(8,128)(2,1)S(1)} %bitcast.152), channel_id=1, source_target_pairs={{0,1},{1,0},{2,3},{3,2},{4,5},{5,4},{6,7},{7,6},{8,9},{9,8},{10,11... | collective-permute-start | bytes 786440 | tf_op jit(solution)/shard_map/ppermute | solution.py:239
  232.9 3.4 collective-permute-start.16
  238.3 310.0 %copy-start.3 = (bf16[128,2880]{0,1:T(8,128)(2,1)}, bf16[128,2880]{0,1:T(8,128)(2,1)S(1)}, u32[]{:S(2)}) copy-start(bf16[128,2880]{0,1:T(8,128)(2,1)S(1)} %get-tuple-element.7) | copy-start | bytes 2211844
  385.3 7.7 %collective-permute-start.17 = (bf16[5,128,2880]{1,2,0:T(8,128)(2,1)}, bf16[5,128,2880]{1,2,0:T(8,128)(2,1)}, u32[]{:S(2)}, u32[]{:S(2)}) collective-permute-start(bf16[5,128,2880]{1,2,0:T(8,128)(2,1)} %copy.142), channel_id=1, source_target_pairs={{0,1},{1,0},{2,3},{3,2},{4,5},{5,4},{6,7},{7,6},{8,9},{9,8},{10,11... | collective-permute-start | bytes 11059208 | tf_op jit(solution)/shard_map/ppermute | solution.py:276
  393.0 23.2 %slice-start = ((s8[6029312]{0:T(1024)(128)(4,1)}), s8[1835008]{0:T(1024)(128)(4,1)S(1)}, s32[]{:S(2)}) async-start(s8[6029312]{0:T(1024)(128)(4,1)} %bitcast.138), calls=%async_computation.3 | async-start | bytes 3670016
  399.6 16.6 %slice-start.1 = ((s8[6029312]{0:T(1024)(128)(4,1)}), s8[4194304]{0:T(1024)(128)(4,1)S(1)}, s32[]{:S(2)}) async-start(s8[6029312]{0:T(1024)(128)(4,1)} %bitcast.138), calls=%async_computation.4 | async-start | bytes 8388608
  399.6 17.1 %slice-start.2 = ((s8[8847360]{0:T(1024)(128)(4,1)}), s8[4194304]{0:T(1024)(128)(4,1)S(1)}, s32[]{:S(2)}) async-start(s8[8847360]{0:T(1024)(128)(4,1)} %bitcast.158), calls=%async_computation.5 | async-start | bytes 8388608
  399.6 17.1 %slice-start.3 = ((s8[8847360]{0:T(1024)(128)(4,1)}), s8[4194304]{0:T(1024)(128)(4,1)S(1)}, s32[]{:S(2)}) async-start(s8[8847360]{0:T(1024)(128)(4,1)} %bitcast.158), calls=%async_computation.6 | async-start | bytes 8388608
  409.6 7.1 %slice-start.4 = ((s8[8847360]{0:T(1024)(128)(4,1)}), s8[458752]{0:T(1024)(128)(4,1)S(1)}, s32[]{:S(2)}) async-start(s8[8847360]{0:T(1024)(128)(4,1)} %bitcast.158), calls=%async_computation.7 | async-start | bytes 917504
  415.7 7.3 %collective-permute-start.18 = (bf16[640,2880]{0,1:T(8,128)(2,1)S(1)}, bf16[640,2880]{0,1:T(8,128)(2,1)}, u32[]{:S(2)}, u32[]{:S(2)}) collective-permute-start(bf16[640,2880]{0,1:T(8,128)(2,1)S(1)} %convolution_convert_fusion), channel_id=1, source_target_pairs={{0,1},{1,0},{2,3},{3,2},{4,5},{5,4},{6,7},{7,6},{8,9},{9,8},{10,11... | collective-permute-start | bytes 11059208 | tf_op jit(solution)/shard_map/ppermute | solution.py:285
  442.9 78.9 %all-to-all-start.1 = ((bf16[5,128,2880]{2,0,1:T(8,128)(2,1)}), bf16[5,128,2880]{2,0,1:T(8,128)(2,1)}, u32[]{:S(2)}, u32[]{:S(2)}) async-start(bf16[5,128,2880]{2,0,1:T(8,128)(2,1)} %copy.145), calls=%async_computation.1 | async-start | bytes 12058624 | tf_op jit(solution)/shard_map/all_to_all | solution.py:287
  542.7 8.7 %copy-start.1 = (bf16[128,2880]{0,1:T(8,128)(2,1)S(1)}, bf16[128,2880]{0,1:T(8,128)(2,1)}, u32[]{:S(2)}) copy-start(bf16[128,2880]{0,1:T(8,128)(2,1)} %param.18) | copy-start | bytes 2211844
  (7 other events, 29.3 us)
Sparse Core Ops, SparseCore 0:
  10.2 170.6 all-gather.2

commit v3 on v1

--- a/solution.py
+++ b/solution.py
@@ -218,24 +218,37 @@
     query_start = jnp.max(
         jnp.where(ends[None, :] <= query_pos[:, None], ends[None, :], 0), axis=1
     ).astype(jnp.int32)
-    local_kv = jnp.concatenate([cache_kv[0], stretch_kv[0]], axis=0)
-    kv_all = lax.all_gather(local_kv, "ctx", axis=0, tiled=False)
-    attended = attention(queries[0], kv_all, cache_rows, sinks, query_pos, query_start, span * ctx_count // 2)
     grp_here = lax.axis_index("grp")
     parity = grp_here % 2
     grp_count = lax.axis_size("grp")
     pair_perm = [(g, g ^ 1) for g in range(grp_count)]
     head_rows = out_proj.shape[0] // 2
-    proj_half = lax.all_gather(
-        lax.dynamic_slice_in_dim(out_proj, parity * head_rows, head_rows, 0), "ctx", axis=0, tiled=True
-    )
+    levels = grp_count // 2
+    level = grp_here // 2
+    sub_rows = head_rows // levels
+    proj_piece = lax.all_gather(
+        lax.dynamic_slice_in_dim(out_proj, parity * head_rows + level * sub_rows, sub_rows, 0), "ctx", axis=0
+    )
+    level_order = (level - jnp.arange(levels, dtype=jnp.int32)) % levels
+    proj_piece, local_kv = lax.optimization_barrier(
+        (proj_piece, jnp.concatenate([cache_kv[0], stretch_kv[0]], axis=0))
+    )
+    kv_all = lax.all_gather(local_kv, "ctx", axis=0, tiled=False)
+    proj_half = jnp.stack(
+        [proj_piece]
+        + [
+            lax.ppermute(proj_piece, "grp", [(g, (g + 2 * k) % grp_count) for g in range(grp_count)])
+            for k in range(1, levels)
+        ]
+    ).reshape(ctx_count * head_rows, -1)
+    attended = attention(queries[0], kv_all, cache_rows, sinks, query_pos, query_start, span * ctx_count // 2)
     by_parity = attended.reshape(tokens, HEADS // 2, 2, HD)
     mine = jnp.where(parity == 0, by_parity[:, :, 0], by_parity[:, :, 1]).reshape(tokens, -1)
     theirs_cols = jnp.where(parity == 0, by_parity[:, :, 1], by_parity[:, :, 0]).reshape(tokens, -1)
     partner_cols = lax.ppermute(theirs_cols, "grp", pair_perm)
-    both = jnp.dot(
-        jnp.concatenate([mine, partner_cols], axis=0), proj_half, preferred_element_type=jnp.float32
-    )
+    stacked = jnp.concatenate([mine, partner_cols], axis=0).reshape(2 * tokens, ctx_count, levels, sub_rows)
+    stacked = jnp.take(stacked, level_order, axis=2).transpose(0, 2, 1, 3).reshape(2 * tokens, -1)
+    both = jnp.dot(stacked, proj_half, preferred_element_type=jnp.float32)
     back = lax.ppermute(both[tokens:], "grp", pair_perm)
     projected = both[:tokens] + back
     mid = (residual[0].astype(jnp.float32) + projected).astype(jnp.bfloat16)

time: 470 us -> 518 us (1.10)
  starting transfers between devices: 8.37 us -> 57.8 us
  blocking collectives: 96.8 us -> 91.4 us
    ppermute x1, starting transfers between devices: 0.09 us -> 45.6 us  [body(): partner_cols = lax.ppermute(theirs_cols, 'grp', pair_perm)]
    all_gather x1, waiting for transfers between devices: 79.3 us -> 70.5 us  [body(): kv_all = lax.all_gather(local_kv, 'ctx', axis=0, tiled=False)]
    all_to_all x1, blocking collectives: 96.8 us -> 91.4 us  [body(): lax.all_to_all(split, ('ctx', 'grp'), split_axis=1, concat_axis=1, tiled=...]
  transfers between devices with their start and end apart: 7 -> 10, of which waited for: 4 -> 4; matrix products, arithmetic and copies ran while one was open for 5% -> 5% of each run, Pallas kernels for 4% -> 3%
where the time goes in v3:
time: 518 us; the launch traced here: 512 us
  waiting for transfers between devices  195 us (38%)
  blocking collectives  91.4 us (18%)
  local copies, waits for them, and re-layouts  82.2 us (16%)
  starting transfers between devices  57.8 us (11%)
  matrix products  35.1 us (7%)
  between operations  22.7 us (4%)
  Pallas kernels  16.5 us (3%)
  other arithmetic  11.7 us (2%)
    all_to_all x1, blocking collectives, body(): lax.all_to_all(split, ('ctx', 'grp'), split_axis=1, concat_axis=1, tiled=...  91.4 us
    all_to_all x1, waiting for transfers between devices, body(): lax.all_to_all(summed.reshape(half_cap, owners, width), ('ctx', 'grp'), s...  72.6 us
    all_gather x1, waiting for transfers between devices, body(): kv_all = lax.all_gather(local_kv, 'ctx', axis=0, tiled=False)  70.5 us
    ppermute x1, starting transfers between devices, body(): partner_cols = lax.ppermute(theirs_cols, 'grp', pair_perm)  45.6 us
    all_gather x1, waiting for transfers between devices, body(): lax.all_gather(lax.dynamic_slice_in_dim(out_proj, parity * head_rows + le...  45.2 us
    gather x8, local copies, waits for them, and re-layouts, body(): expert_rows[pair_dest[:, k]].astype(jnp.float32) * route_weights[:, k:k + 1]  21.3 us
    pallas_call x1, Pallas kernels, flash_all(): pl.pallas_call(kernel, grid_spec=grid_spec, out_shape=jax.ShapeDtypeStruc...  16.5 us
    dot_general x2, matrix products, expert_half(): jnp.dot(rows.reshape(-1, width), in_weights, preferred_element_type=jnp.f...  16.2 us
  transfers between devices with their start and end apart: 10, of which 4 were waited for; matrix products, arithmetic and copies ran while one was open for 5% of the time, Pallas kernels for 3%

profile of v3, /device:TPU:1, one launch (start us, length us, event | category | flops | bytes accessed | tf_op | source)
XLA Modules:
  0.0 512.2 jit_solution(14725368878201526202)
XLA Ops:
  9.5 2.1 pad_maximum_fusion.1
  11.6 45.2 %all-gather.5.cloned.1.call-done = bf16[256,2880]{1,0:T(8,128)(2,1)} async-done(((bf16[16,2880]{1,0:T(8,128)(2,1)}), bf16[256,2880]{1,0:T(8,128)(2,1)}) %all-gather.5.cloned.1.call-update) | async-done | bytes 1474576 | tf_op jit(solution)/shard_map/all_gather | solution.py:229
  67.1 2.0 reshape_reshape.8.sink_ref
  70.7 2.9 copy.211
  75.0 2.6 collective-permute-start.2
  78.7 70.5 %all-gather.7.cloned.1.call-done = bf16[6144,1024]{1,0:T(8,128)(2,1)} async-done(((bf16[384,1024]{1,0:T(8,128)(2,1)}), bf16[6144,1024]{1,0:T(8,128)(2,1)}) %all-gather.7.cloned.1.call-update) | async-done | bytes 12582928 | tf_op jit(solution)/shard_map/all_gather | solution.py:236
  149.2 16.5 %shard_map.131 = bf16[4,1024,128]{2,1,0:T(8,128)(2,1)S(1)} custom-call(s32[4]{0:T(128)S(1)} %pad_add_fusion.s_ref, bf16[4,1024,128]{2,1,0:T(8,128)(2,1)S(1)} %bitcast.108, s32[128,1]{1,0:T(8,128)S(1)} %iota_add_fusion.qpos_ref, s32[128,1]{1,0:T(8,128)S(1)} %copy.173.qstart_ref, f32[4,1024,1]{2,1,0:T(8,128)S(1)} %reshape_reshape.8.sink_ref, ...), custom_call_target="tpu_custom_call" | custom-call | flops 6442450944 | bytes 8388608 | tf_op jit(solution)/shard_map/pallas_call | solution.py:118
  169.7 45.6 %collective-permute-start = (bf16[128,1024]{0,1:T(8,128)(2,1)S(1)}, bf16[128,1024]{0,1:T(8,128)(2,1)S(1)}, u32[]{:S(2)}, u32[]{:S(2)}) collective-permute-start(bf16[128,1024]{0,1:T(8,128)(2,1)S(1)} %bitcast.130), channel_id=1, source_target_pairs={{0,1},{1,0},{2,3},{3,2},{4,5},{5,4},{6,7},{7,6},{8,9},{9,8},{10,11... | collective-permute-start | bytes 786440 | tf_op jit(solution)/shard_map/ppermute | solution.py:248
  217.6 5.7 %fusion.14 = f32[256,2880]{0,1:T(8,128)S(1)} fusion(bf16[1,16,16,2880]{3,1,2,0:T(8,128)(2,1)} %bitcast.32, bf16[1,16,16,2880]{3,1,2,0:T(8,128)(2,1)} %bitcast.31, bf16[1,16,16,2880]{3,1,2,0:T(8,128)(2,1)} %bitcast.30, bf16[1,16,16,2880]{3,1,2,0:T(8,128)(2,1)} %bitcast.107, bf16[4,256,16,16]{1,2,3,0:T(8,128)(2,1)S(1)} %gather_fusion, ...), kind=kOutput, calls=%fused_computation.24 | convolution fusion | flops 1519058944 | bytes 9371652 | tf_op jit(solution)/shard_map/dot_general | solution.py:251
  223.3 1.6 copy-done.4
  226.0 2.4 scatter_custom_fusion
  228.5 2.0 fusion.25
  231.3 4.6 gather_fusion.1
  235.8 4.2 copy.190
  240.0 91.4 %all_to_all.10 = bf16[5,128,2880]{2,0,1:T(8,128)(2,1)} all-to-all(bf16[5,128,2880]{2,0,1:T(8,128)(2,1)S(1)} %copy.190), channel_id=1, replica_groups=mesh['ctx'=16,'grp'=8] {'ctx','grp'}, dimensions={1} | all-to-all | bytes 7372800 | tf_op jit(solution)/shard_map/all_to_all | solution.py:283
  331.5 7.9 %copy.192 = bf16[5,128,2880]{1,2,0:T(8,128)(2,1)} copy(bf16[5,128,2880]{2,0,1:T(8,128)(2,1)} %all_to_all.10) | data formatting | bytes 7372800 | tf_op jit(solution)/shard_map/all_to_all | solution.py:283
  340.6 6.4 %collective-permute-done.5 = bf16[5,128,2880]{1,2,0:T(8,128)(2,1)} collective-permute-done((bf16[5,128,2880]{1,2,0:T(8,128)(2,1)}, bf16[5,128,2880]{1,2,0:T(8,128)(2,1)}, u32[]{:S(2)}, u32[]{:S(2)}) %collective-permute-start.5) | collective-permute-done | bytes 3686432 | tf_op jit(solution)/shard_map/ppermute | solution.py:284
  347.0 6.4 %copy.193 = bf16[5,128,2880]{2,1,0:T(8,128)(2,1)} copy(bf16[5,128,2880]{1,2,0:T(8,128)(2,1)} %collective-permute-done.5) | data formatting | bytes 7372800 | tf_op jit(solution)/shard_map/ppermute | solution.py:284
  353.4 10.0 %fusion = f32[640,1536]{1,0:T(8,128)S(1)} fusion(bf16[640,2880]{1,0:T(8,128)(2,1)} %bitcast.120, bf16[1,2880,1536]{2,1,0:T(8,128)(2,1)} %param.22), kind=kOutput, calls=%fused_computation.7 | convolution fusion | flops 5662310400 | bytes 16465920 | tf_op jit(solution)/shard_map/dot_general | solution.py:287
  363.4 6.1 %convolution_convert_fusion = bf16[640,2880]{0,1:T(8,128)(2,1)S(1)} fusion(bf16[1,768,2880]{1,2,0:T(8,128)(2,1)} %param.23, f32[640,1536]{1,0:T(8,128)S(1)} %fusion), kind=kOutput, calls=%fused_computation.20 | convolution fusion | flops 2836930560 | bytes 12042240 | tf_op jit(solution)/shard_map/dot_general | solution.py:289
  370.5 6.2 %fusion.2 = f32[640,1536]{1,0:T(8,128)S(1)} fusion(bf16[640,2880]{1,0:T(8,128)(2,1)S(1)} %bitcast.121, bf16[1,2880,1536]{2,1,0:T(8,128)(2,1)S(1)} %bitcast.136), kind=kOutput, calls=%fused_computation.9 | convolution fusion | flops 5662310400 | bytes 16465920 | tf_op jit(solution)/shard_map/dot_general | solution.py:287
  376.8 6.9 %add_convert_fusion = bf16[640,2880]{0,1:T(8,128)(2,1)} fusion(bf16[640,2880]{0,1:T(8,128)(2,1)} %collective-permute-done.6, bf16[1,768,2880]{1,2,0:T(8,128)(2,1)S(1)} %bitcast.138, f32[640,1536]{1,0:T(8,128)S(1)} %fusion.2), kind=kOutput, calls=%fused_computation.11 | convolution fusion | flops 2844303360 | bytes 15728640 | tf_op jit(solution)/shard_map/dot_general | solution.py:289
  383.7 6.2 %copy.194 = bf16[640,2880]{1,0:T(8,128)(2,1)} copy(bf16[640,2880]{0,1:T(8,128)(2,1)} %add_convert_fusion) | data formatting | bytes 7372800 | tf_op jit(solution)/shard_map/convert_element_type | solution.py:294
  389.8 6.8 %copy.195 = bf16[5,128,2880]{2,0,1:T(8,128)(2,1)} copy(bf16[5,128,2880]{2,1,0:T(8,128)(2,1)} %bitcast.118) | data formatting | bytes 7372800 | tf_op jit(solution)/shard_map/reshape | solution.py:296
  396.6 5.2 %all-to-all-start.1 = ((bf16[5,128,2880]{2,0,1:T(8,128)(2,1)}), bf16[5,128,2880]{2,0,1:T(8,128)(2,1)}, u32[]{:S(2)}, u32[]{:S(2)}) async-start(bf16[5,128,2880]{2,0,1:T(8,128)(2,1)} %copy.195), calls=%async_computation.1 | async-start | bytes 12058624 | tf_op jit(solution)/shard_map/all_to_all | solution.py:295
  402.9 72.6 %all-to-all-done.1 = bf16[5,128,2880]{2,0,1:T(8,128)(2,1)} async-done(((bf16[5,128,2880]{2,0,1:T(8,128)(2,1)}), bf16[5,128,2880]{2,0,1:T(8,128)(2,1)}, u32[]{:S(2)}, u32[]{:S(2)}) %all-to-all-start.1) | async-done | bytes 3686432 | tf_op jit(solution)/shard_map/all_to_all | solution.py:295
  475.5 5.1 copy.196
  480.6 4.4 gather_fusion.2
  485.4 4.4 gather_fusion.3
  490.9 4.4 gather_fusion.4
  496.4 4.4 gather_fusion.5
  502.0 3.1 fusion.40
  (122 shorter events, 23.9 us)
Async XLA Ops:
  7.2 1.1 copy-start
  7.2 49.6 %copy-start.10 = (s32[1,8]{1,0:T(1,128)S(1)}, s32[1,8]{1,0:T(1,128)}, u32[]{:S(2)}) copy-start(s32[1,8]{1,0:T(1,128)} %param.16) | copy-start | bytes 100
  7.2 58.3 %copy-start.5 = (bf16[1,128,2048]{2,1,0:T(8,128)(2,1)S(1)}, bf16[1,128,2048]{2,1,0:T(8,128)(2,1)}, u32[]{:S(2)}) copy-start(bf16[1,128,2048]{2,1,0:T(8,128)(2,1)} %param.13) | copy-start | bytes 1572868
  7.2 49.6 %all-gather.5.cloned.1.call-start = ((), (), s32[]{:S(2)}) async-start(), calls=%async_computation.2 | async-start | bytes 1601536 | tf_op jit(solution)/shard_map/all_gather | solution.py:229
  9.5 139.7 %all-gather.7.cloned.1.call-start = ((), (), s32[]{:S(2)}) async-start(), calls=%async_computation.3 | async-start | bytes 13369344 | tf_op jit(solution)/shard_map/all_gather | solution.py:236
  65.8 1.1 copy-start.9
  66.0 3.0 copy-start.8
  73.6 144.0 %collective-permute-start.1 = (bf16[16,16,2880]{2,0,1:T(8,128)(2,1)}, bf16[16,16,2880]{2,0,1:T(8,128)(2,1)}, u32[]{:S(2)}, u32[]{:S(2)}) collective-permute-start(bf16[16,16,2880]{2,0,1:T(8,128)(2,1)} %copy.211), channel_id=1, source_target_pairs={{0,2},{1,3},{2,4},{3,5},{4,6},{5,7},{6,0},{7,1},{8,10},{9,11},{10,... | collective-permute-start | bytes 4423688 | tf_op jit(solution)/shard_map/ppermute | solution.py:240
  75.0 142.6 %collective-permute-start.2 = (bf16[16,16,2880]{2,0,1:T(8,128)(2,1)}, bf16[16,16,2880]{2,0,1:T(8,128)(2,1)}, u32[]{:S(2)}, u32[]{:S(2)}) collective-permute-start(bf16[16,16,2880]{2,0,1:T(8,128)(2,1)} %copy.211), channel_id=1, source_target_pairs={{0,4},{1,5},{2,6},{3,7},{4,0},{5,1},{6,2},{7,3},{8,12},{9,13},{10,... | collective-permute-start | bytes 4423688 | tf_op jit(solution)/shard_map/ppermute | solution.py:240
  77.6 140.1 %collective-permute-start.3 = (bf16[16,16,2880]{2,0,1:T(8,128)(2,1)}, bf16[16,16,2880]{2,0,1:T(8,128)(2,1)}, u32[]{:S(2)}, u32[]{:S(2)}) collective-permute-start(bf16[16,16,2880]{2,0,1:T(8,128)(2,1)} %copy.211), channel_id=1, source_target_pairs={{0,6},{1,7},{2,0},{3,1},{4,2},{5,3},{6,4},{7,5},{8,14},{9,15},{10,... | collective-permute-start | bytes 4423688 | tf_op jit(solution)/shard_map/ppermute | solution.py:240
  165.7 1.0 copy-start.2
  169.7 47.1 %collective-permute-start = (bf16[128,1024]{0,1:T(8,128)(2,1)S(1)}, bf16[128,1024]{0,1:T(8,128)(2,1)S(1)}, u32[]{:S(2)}, u32[]{:S(2)}) collective-permute-start(bf16[128,1024]{0,1:T(8,128)(2,1)S(1)} %bitcast.130), channel_id=1, source_target_pairs={{0,1},{1,0},{2,3},{3,2},{4,5},{5,4},{6,7},{7,6},{8,9},{9,8},{10,11... | collective-permute-start | bytes 786440 | tf_op jit(solution)/shard_map/ppermute | solution.py:248
  223.3 1.6 copy-start.4
  225.0 5.4 %copy-start.7 = (f32[2880]{0:T(1024)S(1)}, f32[2880]{0:T(1024)}, u32[]{:S(2)}) copy-start(f32[2880]{0:T(1024)} %param.19) | copy-start | bytes 34564
  225.0 3.4 collective-permute-start.4
  230.4 271.6 %copy-start.3 = (bf16[128,2880]{0,1:T(8,128)(2,1)}, bf16[128,2880]{0,1:T(8,128)(2,1)S(1)}, u32[]{:S(2)}) copy-start(bf16[128,2880]{0,1:T(8,128)(2,1)S(1)} %get-tuple-element.11) | copy-start | bytes 2211844
  339.4 7.7 %collective-permute-start.5 = (bf16[5,128,2880]{1,2,0:T(8,128)(2,1)}, bf16[5,128,2880]{1,2,0:T(8,128)(2,1)}, u32[]{:S(2)}, u32[]{:S(2)}) collective-permute-start(bf16[5,128,2880]{1,2,0:T(8,128)(2,1)} %copy.192), channel_id=1, source_target_pairs={{0,1},{1,0},{2,3},{3,2},{4,5},{5,4},{6,7},{7,6},{8,9},{9,8},{10,11... | collective-permute-start | bytes 11059208 | tf_op jit(solution)/shard_map/ppermute | solution.py:284
  347.0 22.9 %slice-start = ((s8[6029312]{0:T(1024)(128)(4,1)}), s8[1835008]{0:T(1024)(128)(4,1)S(1)}, s32[]{:S(2)}) async-start(s8[6029312]{0:T(1024)(128)(4,1)} %bitcast.113), calls=%async_computation.4 | async-start | bytes 3670016
  353.4 16.6 %slice-start.1 = ((s8[6029312]{0:T(1024)(128)(4,1)}), s8[4194304]{0:T(1024)(128)(4,1)S(1)}, s32[]{:S(2)}) async-start(s8[6029312]{0:T(1024)(128)(4,1)} %bitcast.113), calls=%async_computation.5 | async-start | bytes 8388608
  353.4 17.1 %slice-start.2 = ((s8[8847360]{0:T(1024)(128)(4,1)}), s8[4194304]{0:T(1024)(128)(4,1)S(1)}, s32[]{:S(2)}) async-start(s8[8847360]{0:T(1024)(128)(4,1)} %bitcast.135), calls=%async_computation.6 | async-start | bytes 8388608
  353.4 17.1 %slice-start.3 = ((s8[8847360]{0:T(1024)(128)(4,1)}), s8[4194304]{0:T(1024)(128)(4,1)S(1)}, s32[]{:S(2)}) async-start(s8[8847360]{0:T(1024)(128)(4,1)} %bitcast.135), calls=%async_computation.7 | async-start | bytes 8388608
  363.4 7.1 %slice-start.4 = ((s8[8847360]{0:T(1024)(128)(4,1)}), s8[458752]{0:T(1024)(128)(4,1)S(1)}, s32[]{:S(2)}) async-start(s8[8847360]{0:T(1024)(128)(4,1)} %bitcast.135), calls=%async_computation.8 | async-start | bytes 917504
  369.5 7.3 %collective-permute-start.6 = (bf16[640,2880]{0,1:T(8,128)(2,1)S(1)}, bf16[640,2880]{0,1:T(8,128)(2,1)}, u32[]{:S(2)}, u32[]{:S(2)}) collective-permute-start(bf16[640,2880]{0,1:T(8,128)(2,1)S(1)} %convolution_convert_fusion), channel_id=1, source_target_pairs={{0,1},{1,0},{2,3},{3,2},{4,5},{5,4},{6,7},{7,6},{8,9},{9,8},{10,11... | collective-permute-start | bytes 11059208 | tf_op jit(solution)/shard_map/ppermute | solution.py:293
  370.0 6.8 %slice-start.5 = ((s8[4423680]{0:T(1024)(128)(4,1)}), s8[4194304]{0:T(1024)(128)(4,1)S(1)}, s32[]{:S(2)}) async-start(s8[4423680]{0:T(1024)(128)(4,1)} %bitcast.137), calls=%async_computation.9 | async-start | bytes 8388608
  370.5 6.3 %slice-start.6 = ((s8[4423680]{0:T(1024)(128)(4,1)}), s8[229376]{0:T(1024)(128)(4,1)S(1)}, s32[]{:S(2)}) async-start(s8[4423680]{0:T(1024)(128)(4,1)} %bitcast.137), calls=%async_computation.10 | async-start | bytes 458752
  396.6 5.9 %copy-start.6 = (bf16[2880,64]{0,1:T(8,128)(2,1)S(1)}, bf16[2880,64]{0,1:T(8,128)(2,1)}, u32[]{:S(2)}) copy-start(bf16[2880,64]{0,1:T(8,128)(2,1)} %param.20) | copy-start | bytes 1105924
  396.6 78.9 %all-to-all-start.1 = ((bf16[5,128,2880]{2,0,1:T(8,128)(2,1)}), bf16[5,128,2880]{2,0,1:T(8,128)(2,1)}, u32[]{:S(2)}, u32[]{:S(2)}) async-start(bf16[5,128,2880]{2,0,1:T(8,128)(2,1)} %copy.195), calls=%async_computation.1 | async-start | bytes 12058624 | tf_op jit(solution)/shard_map/all_to_all | solution.py:295
  496.4 8.7 %copy-start.1 = (bf16[128,2880]{0,1:T(8,128)(2,1)S(1)}, bf16[128,2880]{0,1:T(8,128)(2,1)}, u32[]{:S(2)}) copy-start(bf16[128,2880]{0,1:T(8,128)(2,1)} %param.18) | copy-start | bytes 2211844
Sparse Core Ops, SparseCore 0:
  10.8 45.9 all-gather.4
  58.9 90.2 all-gather.6
